TPU v7x, 256 devices: a whole 4x4x8 slice. The times are simulated.
256 devices in a mesh: wide: 64 (over z, x, y_lo), narrow: 4 (over y_hi, core).
Axes of the slice: x: 4, y: 4 (y_hi: 2, y_lo: 2; y = y_hi * 2 + y_lo), z: 8, core: 2. Of those that a mesh axis runs over, the one named last changes fastest.
Arguments:
- density: bfloat16 [8192, 8, 128], P(('wide', 'narrow')), may hold values from -6 to 6
- basis: bfloat16 [8192, 64, 128], P(('wide', 'narrow')), may hold values from -0.5 to 0.5
- near_list: int32 [8192, 6], P(('wide', 'narrow')), may hold values from 0 to 8191, as said below
- near_blocks: bfloat16 [8192, 6, 128, 128], P(('wide', 'narrow')), may hold values from -0.21875 to 0.21875
- far_leaf: int32 [8192, 6], P(('wide', 'narrow')), may hold values from 0 to 8191, as said below
- leaf_coupling: bfloat16 [8192, 64, 384], P(('wide', 'narrow')), may hold values from -0.3125 to 0.3125
- transfer: bfloat16 [1024, 64, 512], P(('wide', 'narrow')), may hold values from -0.75 to 0.75
- far_coarse: int32 [1024, 8], P(('wide', 'narrow')), may hold values from 0 to 1023
- coarse_coupling: bfloat16 [1024, 64, 512], P(('wide', 'narrow')), may hold values from -0.25 to 0.25
Outputs:
- potential: bfloat16 [8192, 8, 128], P(('wide', 'narrow'))
Inputs may be any that keep to these rules, and one draw needn't show every extreme that they name: `near_list`: every entry lies within 32 leaves of its own leaf l; the first entry is l itself. `far_leaf`: every entry lies within 32 leaves of its own leaf.
All inputs are finite; a program needn't handle non-finite values.
Results may differ from a plain program's by a relative error of at most 0.0066.
Values may be sent and summed in bfloat16 or wider, within the bound.
No kernel may reach another device: no remote copies, remote signals or barrier semaphores. Data moves between devices by JAX's collectives and lax.ppermute only.
A program may use at most 64 MiB of HBM per device.

v0:
```python
import jax
import jax.numpy as jnp
from jax import lax
from jax.sharding import Mesh, PartitionSpec as P


ALL = ("z", "x", "y_lo", "y_hi", "core")
STAGES = (("x", "y_lo", "y_hi"), ("z",))
PAIR = "core"


def with_halo(block, sides, width):
    for axis, dim in sides:
        count = lax.axis_size(axis)
        forward = [(i, i + 1) for i in range(count - 1)]
        backward = [(target, source) for source, target in forward]
        low = lax.ppermute(
            lax.slice_in_dim(block, block.shape[dim] - width, None, axis=dim), axis, forward
        )
        high = lax.ppermute(lax.slice_in_dim(block, 0, width, axis=dim), axis, backward)
        block = jnp.concatenate([low, block, high], axis=dim)
    return block


def side_by_side(parts):
    n, j, r, m = parts.shape
    return parts.transpose(0, 2, 1, 3).reshape(n, r, j * m)


def body(
    density,
    basis,
    near_list,
    near_blocks,
    far_leaf,
    leaf_coupling,
    transfer,
    far_coarse,
    coarse_coupling,
):
    leaf_count, rhs_count, leaf_width = density.shape
    rank_width = basis.shape[1]
    box_count = transfer.shape[0]
    child_count = leaf_count // box_count
    far_count = far_leaf.shape[1]
    coarse_count = far_coarse.shape[1]
    skeleton = jnp.einsum(
        "lrp,lkp->lrk", density, basis, preferred_element_type=jnp.float32
    ).astype(jnp.bfloat16)
    children = skeleton.reshape(box_count, child_count, rhs_count, rank_width)
    coarse = jnp.einsum(
        "ckq,crq->crk", transfer, side_by_side(children), preferred_element_type=jnp.float32
    ).astype(jnp.bfloat16)
    coarse_flat = coarse.reshape(box_count, rhs_count * rank_width)
    everything = coarse_flat
    for axes in STAGES:
        n = lax.axis_size(axes)
        spread = jnp.broadcast_to(everything[None], (n,) + everything.shape)
        moved = lax.all_to_all(spread, axes, 0, 0, tiled=False)
        everything = moved.reshape(
            (n * everything.shape[0],) + everything.shape[1:]
        )
    offset_base = lax.axis_index(ALL) * leaf_count - leaf_count
    partner_far = lax.ppermute(far_coarse, PAIR, [(0, 1), (1, 0)])
    density_flat = density.reshape(leaf_count, rhs_count * leaf_width)
    skeleton_flat = skeleton.reshape(leaf_count, rhs_count * rank_width)
    both_padded = with_halo(
        jnp.concatenate([density_flat, skeleton_flat], axis=1), ((ALL, 0),), leaf_count
    )
    density_padded = both_padded[:, : density_flat.shape[1]]
    skeleton_padded = both_padded[:, density_flat.shape[1] :]
    near_rows = jnp.take(density_padded, near_list - offset_base, axis=0).reshape(
        leaf_count, near_list.shape[1], rhs_count, leaf_width
    )
    near_part = jnp.einsum(
        "ljpq,ljrq->lrp", near_blocks, near_rows, preferred_element_type=jnp.float32
    )
    far_skels = jnp.take(skeleton_padded, far_leaf - offset_base, axis=0).reshape(
        leaf_count, far_count, rhs_count, rank_width
    )
    leaf_far = jnp.einsum(
        "lkq,lrq->lrk", leaf_coupling, side_by_side(far_skels), preferred_element_type=jnp.float32
    )
    everything, near_part, leaf_far = lax.optimization_barrier((everything, near_part, leaf_far))
    def placed(boxes):
        owner, slot = boxes // box_count, boxes % box_count
        coords = {}
        for a in reversed(ALL):
            coords[a] = owner % lax.axis_size(a)
            owner = owner // lax.axis_size(a)
        position = 0
        for axes in reversed(STAGES):
            for a in axes:
                position = position * lax.axis_size(a) + coords[a]
        return position * box_count + slot, coords[PAIR] != lax.axis_index(PAIR)

    row, elsewhere = placed(far_coarse)
    asked, _ = placed(partner_far)
    served = lax.ppermute(jnp.take(everything, asked, axis=0), PAIR, [(0, 1), (1, 0)])
    coarse_skels = jnp.where(
        elsewhere[:, :, None], served, jnp.take(everything, row, axis=0)
    ).reshape(box_count, coarse_count, rhs_count, rank_width)
    coarse_field = jnp.einsum(
        "ckq,crq->crk", coarse_coupling, side_by_side(coarse_skels), preferred_element_type=jnp.float32
    ).astype(jnp.bfloat16)
    descended = jnp.einsum(
        "crk,ckq->crq", coarse_field, transfer, preferred_element_type=jnp.float32
    )
    descended = (
        descended.reshape(box_count, rhs_count, child_count, rank_width)
        .transpose(0, 2, 1, 3)
        .reshape(leaf_count, rhs_count, rank_width)
    )
    local_field = (leaf_far + descended).astype(jnp.bfloat16)
    total = (
        jnp.einsum("lrk,lkp->lrp", local_field, basis, preferred_element_type=jnp.float32)
        + near_part
    )
    return total.astype(jnp.bfloat16)


def solution(mesh):
    assert tuple(mesh.shape.values()) == (64, 4)
    grid = Mesh(mesh.devices.reshape(8, 4, 2, 2, 2), ALL)
    return jax.shard_map(
        body,
        mesh=grid,
        in_specs=(
            P(ALL, None, None),
            P(ALL, None, None),
            P(ALL, None),
            P(ALL, None, None, None),
            P(ALL, None),
            P(ALL, None, None),
            P(ALL, None, None),
            P(ALL, None),
            P(ALL, None, None),
        ),
        out_specs=P(ALL, None, None),
        check_vma=False,
    )
```

profile of v0, /device:TPU:1, one launch (start us, length us, event | category | flops | bytes accessed | tf_op | source)
XLA Modules:
  0.0 55.5 jit_solution(14576628246749807163)
XLA Ops:
  0.0 1.6 %convolution_convert_fusion = bf16[32,8,64]{2,1,0:T(8,128)(2,1)S(1)} fusion(bf16[32,8,128]{2,1,0:T(8,128)(2,1)} %param.11, bf16[32,64,128]{2,1,0:T(8,128)(2,1)} %param.12), kind=kOutput, calls=%fused_computation.7 | convolution fusion | flops 4210688 | bytes 622592 | tf_op jit(solution)/shard_map/lrp,lkp->lrk/dot_general | solution.py:47
  1.7 0.9 %bitcast_dynamic-update-slice_fusion = bf16[32,1536]{1,0:T(8,128)(2,1)S(1)} fusion(bf16[4,8,8,128]{3,2,1,0:T(8,128)(2,1)} %bitcast.49), kind=kLoop, calls=%fused_computation.20 | loop fusion | bytes 131072
  2.6 6.2 %collective-permute-start = (bf16[32,1536]{1,0:T(8,128)(2,1)S(1)}, bf16[32,1536]{1,0:T(8,128)(2,1)S(1)}, u32[]{:S(2)}, u32[]{:S(2)}) collective-permute-start(bf16[32,1536]{1,0:T(8,128)(2,1)S(1)} %constant_dynamic-update-slice_fusion), channel_id=1, source_target_pairs={{0,1},{1,2},{2,3},{3,4},{4,5},{5,6},{6,7},{7,8},{8,9},{9,10},{10,1... | collective-permute-start | bytes 294920 | tf_op jit(solution)/shard_map/ppermute | solution.py:17
  8.8 1.9 %collective-permute-start.1 = (bf16[32,1536]{1,0:T(8,128)(2,1)S(1)}, bf16[32,1536]{1,0:T(8,128)(2,1)}, u32[]{:S(2)}, u32[]{:S(2)}) collective-permute-start(bf16[32,1536]{1,0:T(8,128)(2,1)S(1)} %constant_dynamic-update-slice_fusion), channel_id=1, source_target_pairs={{1,0},{2,1},{3,2},{4,3},{5,4},{6,5},{7,6},{8,7},{9,8},{10,9},{11,1... | collective-permute-start | bytes 294920 | tf_op jit(solution)/shard_map/ppermute | solution.py:20
  10.8 1.1 %convolution_convert_fusion.2 = bf16[4,8,64]{2,1,0:T(8,128)(2,1)S(1)} fusion(bf16[4,8,512]{2,1,0:T(8,128)(2,1)S(1)} %reshape.53, bf16[4,64,512]{2,1,0:T(8,128)(2,1)} %param.17), kind=kOutput, calls=%fused_computation.9 | convolution fusion | flops 2099200 | bytes 299008 | tf_op jit(solution)/shard_map/ckq,crq->crk/dot_general | solution.py:51
  12.1 0.7 %broadcast_in_dim.57 = bf16[16,4,512]{2,1,0:T(4,128)(2,1)} broadcast(bf16[4,512]{1,0:T(4,128)(2,1)S(1)} %broadcast_in_dim.56), dimensions={1,2} | broadcast | bytes 69632 | tf_op jit(solution)/shard_map/broadcast_in_dim | solution.py:58
  12.7 4.6 %all-to-all-start = ((bf16[16,4,512]{2,1,0:T(4,128)(2,1)}), bf16[16,4,512]{2,1,0:T(4,128)(2,1)S(1)}, u32[]{:S(2)}, u32[]{:S(2)}) async-start(bf16[16,4,512]{2,1,0:T(4,128)(2,1)} %broadcast_in_dim.57), calls=%async_computation | async-start | bytes 131072 | tf_op jit(solution)/shard_map/all_to_all | solution.py:59
  17.3 3.0 %collective-permute-start.2 = (s32[4,8]{1,0:T(4,128)}, s32[4,8]{1,0:T(4,128)S(1)}, u32[]{:S(2)}, u32[]{:S(2)}) collective-permute-start(s32[4,8]{1,0:T(4,128)} %param.18), channel_id=1, source_target_pairs={{0,1},{1,0},{2,3},{3,2},{4,5},{5,4},{6,7},{7,6},{8,9},{9,8},{10,11... | collective-permute-start | bytes 392 | tf_op jit(solution)/shard_map/ppermute | solution.py:64
  20.3 0.7 %compare_and_fusion.2 = (pred[4,8]{1,0:T(4,128)(4,1)S(1)}, s32[4,8]{1,0:T(4,128)S(1)}, pred[4,8]{1,0:T(4,128)(4,1)S(1)}) fusion(s32[4,8]{1,0:T(4,128)} %param.18, s32[]{:T(128)S(6)} %axis_index.56), kind=kLoop, calls=%fused_computation.130 | loop fusion | flops 3872 | bytes 324 | tf_op jit(solution)/shard_map/jit(_take)/and | solution.py:101
  21.0 0.7 %compare_and_fusion = (pred[32,6]{0,1:T(8,128)(4,1)S(1)}, s32[32,6]{0,1:T(8,128)S(1)}, pred[32,6]{0,1:T(8,128)(4,1)S(1)}, s32[32,6]{0,1:T(8,128)S(1)}) fusion(s32[32,6]{0,1:T(8,128)} %param.15, s32[]{:T(128)S(6)} %sub.55, s32[32,6]{0,1:T(8,128)} %param.13), kind=kLoop, calls=%fused_computation.33 | loop fusion | flops 2688 | bytes 3460 | tf_op jit(solution)/shard_map/jit(_take)/and | solution.py:78
  22.6 1.5 %all-to-all-done = bf16[16,4,512]{2,1,0:T(4,128)(2,1)S(1)} async-done(((bf16[16,4,512]{2,1,0:T(4,128)(2,1)}), bf16[16,4,512]{2,1,0:T(4,128)(2,1)S(1)}, u32[]{:S(2)}, u32[]{:S(2)}) %all-to-all-start) | async-done | bytes 65568 | tf_op jit(solution)/shard_map/all_to_all | solution.py:59
  24.1 0.8 %broadcast_in_dim.59 = bf16[8,64,512]{2,1,0:T(8,128)(2,1)} broadcast(bf16[64,512]{1,0:T(8,128)(2,1)S(1)} %broadcast_in_dim.58), dimensions={1,2} | broadcast | bytes 589824 | tf_op jit(solution)/shard_map/broadcast_in_dim | solution.py:58
  24.9 7.8 %all-to-all-start.1 = ((bf16[8,64,512]{2,1,0:T(8,128)(2,1)}), bf16[8,64,512]{2,1,0:T(8,128)(2,1)S(1)}, u32[]{:S(2)}, u32[]{:S(2)}) async-start(bf16[8,64,512]{2,1,0:T(8,128)(2,1)} %broadcast_in_dim.59), calls=%async_computation.1 | async-start | bytes 1048576 | tf_op jit(solution)/shard_map/all_to_all | solution.py:59
  32.8 0.8 %pad_maximum_fusion.1 = bf16[96,512]{1,0:T(8,128)(2,1)S(1)} fusion(bf16[32,1536]{1,0:T(8,128)(2,1)} %collective-permute-done.1, bf16[32,1536]{1,0:T(8,128)(2,1)S(1)} %constant_dynamic-update-slice_fusion, bf16[32,1536]{1,0:T(8,128)(2,1)S(1)} %collective-permute-done), kind=kLoop, calls=%fused_computation.19 | loop fusion | flops 294912 | bytes 393216 | tf_op jit(solution)/shard_map/slice | solution.py:71
  33.5 1.0 %gather_fusion.1 = bf16[192,512]{1,0:T(8,128)(2,1)S(1)} fusion(bf16[96,512]{1,0:T(8,128)(2,1)S(1)} %pad_maximum_fusion.1, s32[1024]{0:T(1024)S(1)} %pad_clamp_fusion.2), kind=kCustom, calls=%fused_computation.3 | custom fusion | bytes 393984 | tf_op jit(solution)/shard_map/jit(_take)/gather | solution.py:78
  35.2 0.9 %pad_maximum_fusion = bf16[96,1536]{1,0:T(8,128)(2,1)S(1)} fusion(bf16[32,1536]{1,0:T(8,128)(2,1)} %collective-permute-done.1, bf16[32,1536]{1,0:T(8,128)(2,1)S(1)} %constant_dynamic-update-slice_fusion, bf16[32,1536]{1,0:T(8,128)(2,1)S(1)} %collective-permute-done), kind=kLoop, calls=%fused_computation.15 | loop fusion | flops 884736 | bytes 589824 | tf_op jit(solution)/shard_map/concatenate | solution.py:21
  36.2 1.0 %gather_fusion = bf16[192,1024]{1,0:T(8,128)(2,1)S(1)} fusion(bf16[96,1024]{1,0:T(8,128)(2,1)S(1)} %slice.16, s32[1024]{0:T(1024)S(1)} %pad_clamp_fusion.3), kind=kCustom, calls=%fused_computation.2 | custom fusion | bytes 787200 | tf_op jit(solution)/shard_map/jit(_take)/gather | solution.py:72
  37.3 0.6 %fusion.39 = f32[32,8,64]{2,1,0:T(8,128)S(1)} fusion(bf16[32,8,384]{2,1,0:T(8,128)(2,1)S(1)} %reshape.57, bf16[32,64,384]{2,1,0:T(8,128)(2,1)S(1)} %copy-done), kind=kOutput, calls=%fused_computation.135 | convolution fusion | flops 12582912 | bytes 1835008 | tf_op jit(solution)/shard_map/lkq,lrq->lrk/dot_general | solution.py:81
  37.9 4.6 %convolution_bitcast_fusion = f32[32,8,128]{2,1,0:T(8,128)S(1)} fusion(bf16[32,6,128,128]{3,2,1,0:T(8,128)(2,1)} %param.14, bf16[32,6,8,128]{3,2,1,0:T(8,128)(2,1)S(1)} %bitcast.47, pred[32,6]{1,0:T(8,128)(4,1)S(1)} %copy.23), kind=kOutput, calls=%fused_computation.5 | convolution fusion | flops 50528256 | bytes 6815936 | tf_op jit(solution)/shard_map/ljpq,ljrq->lrp/dot_general | solution.py:75
  42.5 2.3 %all-to-all-done.1 = bf16[8,64,512]{2,1,0:T(8,128)(2,1)S(1)} async-done(((bf16[8,64,512]{2,1,0:T(8,128)(2,1)}), bf16[8,64,512]{2,1,0:T(8,128)(2,1)S(1)}, u32[]{:S(2)}, u32[]{:S(2)}) %all-to-all-start.1) | async-done | bytes 524320 | tf_op jit(solution)/shard_map/all_to_all | solution.py:59
  44.8 0.6 %gather_fusion.2 = bf16[32,512]{1,0:T(8,128)(2,1)S(1)} fusion(bf16[512,512]{1,0:T(8,128)(2,1)S(1)} %bitcast.45, s32[1024]{0:T(1024)S(1)} %pad_clamp_fusion.1), kind=kCustom, calls=%fused_computation.clone | custom fusion | bytes 65664 | tf_op jit(solution)/shard_map/jit(_take)/gather | solution.py:99
  45.5 6.4 %collective-permute-start.3 = (bf16[4,8,512]{2,1,0:T(8,128)(2,1)S(1)}, bf16[4,8,512]{2,1,0:T(8,128)(2,1)S(1)}, u32[]{:S(2)}, u32[]{:S(2)}) collective-permute-start(bf16[4,8,512]{2,1,0:T(8,128)(2,1)S(1)} %bitcast_select_fusion.1), channel_id=1, source_target_pairs={{0,1},{1,0},{2,3},{3,2},{4,5},{5,4},{6,7},{7,6},{8,9},{9,8},{10,11... | collective-permute-start | bytes 98312 | tf_op jit(solution)/shard_map/ppermute | solution.py:99
  53.2 1.2 %fusion.1 = f32[4,8,512]{2,1,0:T(8,128)S(1)} fusion(bf16[4,64,512]{2,1,0:T(8,128)(2,1)S(1)} %copy-done.2, bf16[4,8,512]{2,1,0:T(8,128)(2,1)S(1)} %reshape.59, bf16[4,64,512]{2,1,0:T(8,128)(2,1)} %param.19), kind=kOutput, calls=%fused_computation.10 | convolution fusion | flops 4196352 | bytes 622592 | tf_op jit(solution)/shard_map/crk,ckq->crq/dot_general | solution.py:106
  54.6 0.9 %fusion = bf16[32,8,128]{2,1,0:T(8,128)(2,1)} fusion(f32[32,8,128]{2,1,0:T(8,128)S(1)} %convolution_bitcast_fusion, bf16[32,8,64]{2,1,0:T(8,128)(2,1)S(1)} %fusion.6, bf16[32,64,128]{2,1,0:T(8,128)(2,1)S(1)} %copy-done.1), kind=kOutput, calls=%fused_computation.6 | convolution fusion | flops 4259840 | bytes 753664 | tf_op jit(solution)/shard_map/lrk,lkp->lrp/dot_general | solution.py:116
  (43 shorter events, 3.4 us)
Async XLA Ops:
  0.0 37.3 %copy-start = (bf16[32,64,384]{2,1,0:T(8,128)(2,1)S(1)}, bf16[32,64,384]{2,1,0:T(8,128)(2,1)}, u32[]{:S(2)}) copy-start(bf16[32,64,384]{2,1,0:T(8,128)(2,1)} %param.16) | copy-start | bytes 4718596
  2.6 30.2 %collective-permute-start = (bf16[32,1536]{1,0:T(8,128)(2,1)S(1)}, bf16[32,1536]{1,0:T(8,128)(2,1)S(1)}, u32[]{:S(2)}, u32[]{:S(2)}) collective-permute-start(bf16[32,1536]{1,0:T(8,128)(2,1)S(1)} %constant_dynamic-update-slice_fusion), channel_id=1, source_target_pairs={{0,1},{1,2},{2,3},{3,4},{4,5},{5,6},{6,7},{7,8},{8,9},{9,10},{10,1... | collective-permute-start | bytes 294920 | tf_op jit(solution)/shard_map/ppermute | solution.py:17
  8.8 24.0 %collective-permute-start.1 = (bf16[32,1536]{1,0:T(8,128)(2,1)S(1)}, bf16[32,1536]{1,0:T(8,128)(2,1)}, u32[]{:S(2)}, u32[]{:S(2)}) collective-permute-start(bf16[32,1536]{1,0:T(8,128)(2,1)S(1)} %constant_dynamic-update-slice_fusion), channel_id=1, source_target_pairs={{1,0},{2,1},{3,2},{4,3},{5,4},{6,5},{7,6},{8,7},{9,8},{10,9},{11,1... | collective-permute-start | bytes 294920 | tf_op jit(solution)/shard_map/ppermute | solution.py:20
  12.7 11.3 %all-to-all-start = ((bf16[16,4,512]{2,1,0:T(4,128)(2,1)}), bf16[16,4,512]{2,1,0:T(4,128)(2,1)S(1)}, u32[]{:S(2)}, u32[]{:S(2)}) async-start(bf16[16,4,512]{2,1,0:T(4,128)(2,1)} %broadcast_in_dim.57), calls=%async_computation | async-start | bytes 131072 | tf_op jit(solution)/shard_map/all_to_all | solution.py:59
  17.3 5.1 %collective-permute-start.2 = (s32[4,8]{1,0:T(4,128)}, s32[4,8]{1,0:T(4,128)S(1)}, u32[]{:S(2)}, u32[]{:S(2)}) collective-permute-start(s32[4,8]{1,0:T(4,128)} %param.18), channel_id=1, source_target_pairs={{0,1},{1,0},{2,3},{3,2},{4,5},{5,4},{6,7},{7,6},{8,9},{9,8},{10,11... | collective-permute-start | bytes 392 | tf_op jit(solution)/shard_map/ppermute | solution.py:64
  24.9 19.9 %all-to-all-start.1 = ((bf16[8,64,512]{2,1,0:T(8,128)(2,1)}), bf16[8,64,512]{2,1,0:T(8,128)(2,1)S(1)}, u32[]{:S(2)}, u32[]{:S(2)}) async-start(bf16[8,64,512]{2,1,0:T(8,128)(2,1)} %broadcast_in_dim.59), calls=%async_computation.1 | async-start | bytes 1048576 | tf_op jit(solution)/shard_map/all_to_all | solution.py:59
  37.2 16.0 %copy-start.2 = (bf16[4,64,512]{2,1,0:T(8,128)(2,1)S(1)}, bf16[4,64,512]{2,1,0:T(8,128)(2,1)}, u32[]{:S(2)}) copy-start(bf16[4,64,512]{2,1,0:T(8,128)(2,1)} %param.17) | copy-start | bytes 786436
  37.2 17.4 %copy-start.1 = (bf16[32,64,128]{2,1,0:T(8,128)(2,1)S(1)}, bf16[32,64,128]{2,1,0:T(8,128)(2,1)}, u32[]{:S(2)}) copy-start(bf16[32,64,128]{2,1,0:T(8,128)(2,1)} %param.12) | copy-start | bytes 1572868
  45.5 7.3 %collective-permute-start.3 = (bf16[4,8,512]{2,1,0:T(8,128)(2,1)S(1)}, bf16[4,8,512]{2,1,0:T(8,128)(2,1)S(1)}, u32[]{:S(2)}, u32[]{:S(2)}) collective-permute-start(bf16[4,8,512]{2,1,0:T(8,128)(2,1)S(1)} %bitcast_select_fusion.1), channel_id=1, source_target_pairs={{0,1},{1,0},{2,3},{3,2},{4,5},{5,4},{6,7},{7,6},{8,9},{9,8},{10,11... | collective-permute-start | bytes 98312 | tf_op jit(solution)/shard_map/ppermute | solution.py:99
where the time goes:
time: 56 us; the launch traced here: 55.5 us
  starting transfers between devices  29.9 us (53%)
  matrix products  9.99 us (18%)
  local copies, waits for them, and re-layouts  7.75 us (14%)
  waiting for transfers between devices  4.03 us (7%)
  other arithmetic  3.52 us (6%)
    all_to_all x2, starting transfers between devices, body(): moved = lax.all_to_all(spread, axes, 0, 0, tiled=False)  12.4 us
    ppermute x1, starting transfers between devices, body(): lax.ppermute(jnp.take(everything, asked, axis=0), PAIR, [(0, 1), (1, 0)])  6.44 us
    ppermute x1, starting transfers between devices, with_halo(): lax.ppermute(lax.slice_in_dim(block, block.shape[dim] - width, None, axis...  6.2 us
    dot_general x1, matrix products, body(): jnp.einsum('ljpq,ljrq->lrp', near_blocks, near_rows, preferred_element_ty...  4.56 us
    all_to_all x2, waiting for transfers between devices, body(): moved = lax.all_to_all(spread, axes, 0, 0, tiled=False)  3.79 us
    ppermute x1, starting transfers between devices, body(): partner_far = lax.ppermute(far_coarse, PAIR, [(0, 1), (1, 0)])  2.95 us
    ppermute x1, starting transfers between devices, with_halo(): lax.ppermute(lax.slice_in_dim(block, 0, width, axis=dim), axis, backward)  1.92 us
    broadcast_in_dim x4, local copies, waits for them, and re-layouts, body(): spread = jnp.broadcast_to(everything[None], (n,) + everything.shape)  1.62 us
  transfers between devices with their start and end apart: 6, of which 3 were waited for; matrix products, arithmetic and copies ran while one was open for 28% of the time, Pallas kernels for 0%

commit v1 on v0

--- a/solution.py
+++ b/solution.py
@@ -5,21 +5,8 @@
 
 
 ALL = ("z", "x", "y_lo", "y_hi", "core")
-STAGES = (("x", "y_lo", "y_hi"), ("z",))
+STAGES = (("z",), ("x", "y_lo", "y_hi"))
 PAIR = "core"
-
-
-def with_halo(block, sides, width):
-    for axis, dim in sides:
-        count = lax.axis_size(axis)
-        forward = [(i, i + 1) for i in range(count - 1)]
-        backward = [(target, source) for source, target in forward]
-        low = lax.ppermute(
-            lax.slice_in_dim(block, block.shape[dim] - width, None, axis=dim), axis, forward
-        )
-        high = lax.ppermute(lax.slice_in_dim(block, 0, width, axis=dim), axis, backward)
-        block = jnp.concatenate([low, block, high], axis=dim)
-    return block
 
 
 def side_by_side(parts):
@@ -60,28 +47,48 @@
         everything = moved.reshape(
             (n * everything.shape[0],) + everything.shape[1:]
         )
-    offset_base = lax.axis_index(ALL) * leaf_count - leaf_count
-    partner_far = lax.ppermute(far_coarse, PAIR, [(0, 1), (1, 0)])
     density_flat = density.reshape(leaf_count, rhs_count * leaf_width)
     skeleton_flat = skeleton.reshape(leaf_count, rhs_count * rank_width)
-    both_padded = with_halo(
-        jnp.concatenate([density_flat, skeleton_flat], axis=1), ((ALL, 0),), leaf_count
+    device_count = lax.axis_size(ALL)
+    me = lax.axis_index(ALL)
+    even = lax.axis_index(PAIR) == 0
+    own = jnp.concatenate([density_flat, skeleton_flat], axis=1)
+    width = own.shape[1]
+    digits = jnp.stack([far_coarse // 32, far_coarse % 32]).reshape(1, -1).astype(own.dtype)
+    extra = jnp.pad(digits, ((0, 0), (0, width - digits.shape[1])))
+    cross_pairs = [(d, d + 1) for d in range(1, device_count - 1, 2)]
+    cross_pairs += [(d + 1, d) for d in range(1, device_count - 1, 2)]
+    cross = lax.ppermute(own, ALL, cross_pairs)
+    received = lax.ppermute(
+        jnp.concatenate([own, extra], axis=0), PAIR, [(0, 1), (1, 0)]
     )
-    density_padded = both_padded[:, : density_flat.shape[1]]
-    skeleton_padded = both_padded[:, density_flat.shape[1] :]
-    near_rows = jnp.take(density_padded, near_list - offset_base, axis=0).reshape(
+    pair_halo = received[:leaf_count]
+    got = received[leaf_count, : digits.shape[1]].astype(jnp.int32).reshape(2, *far_coarse.shape)
+    partner_far = got[0] * 32 + got[1]
+    padded = jnp.concatenate([pair_halo, own, cross], axis=0)
+    density_padded = padded[:, : density_flat.shape[1]]
+    skeleton_padded = padded[:, density_flat.shape[1] :]
+
+    def halo_row(index):
+        t = index - me * leaf_count
+        low = jnp.where(even, t + 3 * leaf_count, t + leaf_count)
+        high = jnp.where(even, t - leaf_count, t + leaf_count)
+        return jnp.where(t < 0, low, jnp.where(t < leaf_count, t + leaf_count, high))
+
+    near_rows = jnp.take(density_padded, halo_row(near_list), axis=0).reshape(
         leaf_count, near_list.shape[1], rhs_count, leaf_width
     )
     near_part = jnp.einsum(
         "ljpq,ljrq->lrp", near_blocks, near_rows, preferred_element_type=jnp.float32
     )
-    far_skels = jnp.take(skeleton_padded, far_leaf - offset_base, axis=0).reshape(
+    far_skels = jnp.take(skeleton_padded, halo_row(far_leaf), axis=0).reshape(
         leaf_count, far_count, rhs_count, rank_width
     )
     leaf_far = jnp.einsum(
         "lkq,lrq->lrk", leaf_coupling, side_by_side(far_skels), preferred_element_type=jnp.float32
     )
     everything, near_part, leaf_far = lax.optimization_barrier((everything, near_part, leaf_far))
+
     def placed(boxes):
         owner, slot = boxes // box_count, boxes % box_count
         coords = {}

time: 56 us -> 44 us (0.79)
  starting transfers between devices: 29.9 us -> 22.2 us
  waiting for transfers between devices: 4.03 us -> 0.78 us
  other arithmetic: 3.52 us -> 2.67 us
    ppermute x3 -> x2, starting transfers between devices: 11.1 us -> 5.76 us  [the longest x1 5.66 us: body(): cross = lax.ppermute(own, ALL, cross_pairs)]
    ppermute x1, starting transfers between devices: 6.44 us -> 2.71 us  [body(): lax.ppermute(jnp.take(everything, asked, axis=0), PAIR, [(0, 1), (1, 0)])]
    all_to_all x2, waiting for transfers between devices: 3.79 us -> 0.55 us  [body(): moved = lax.all_to_all(spread, axes, 0, 0, tiled=False)]
    all_to_all x2, starting transfers between devices: 12.4 us -> 13.7 us  [body(): moved = lax.all_to_all(spread, axes, 0, 0, tiled=False)]
    dot_general x1, matrix products: 1.24 us -> 0.29 us  [body(): jnp.einsum('crk,ckq->crq', coarse_field, transfer, preferred_element_type...]
    concatenate x1 -> x2, other arithmetic: 0.91 us -> 0.03 us  [the longest x1 0.02 us: body(): padded = jnp.concatenate([pair_halo, own, cross], axis=0)]
    slice x1, other arithmetic: 0.77 us -> 0.01 us  [body(): skeleton_padded = padded[:, density_flat.shape[1]:]]
    another operation x0 -> x2, other arithmetic: none -> 0.71 us  [body(): jnp.stack([far_coarse // 32, far_coarse % 32]).reshape(1, -1)]
  transfers between devices with their start and end apart: 6 -> 5, of which waited for: 3 -> 2; matrix products, arithmetic and copies ran while one was open for 28% -> 33% of each run, Pallas kernels for 0% -> 0%
where the time goes in v1:
time: 44 us; the launch traced here: 43.6 us
  starting transfers between devices  22.2 us (50%)
  matrix products  9.73 us (22%)
  local copies, waits for them, and re-layouts  7.92 us (18%)
  other arithmetic  2.67 us (6%)
  waiting for transfers between devices  0.78 us (2%)
    all_to_all x2, starting transfers between devices, body(): moved = lax.all_to_all(spread, axes, 0, 0, tiled=False)  13.7 us
    ppermute x1, starting transfers between devices, body(): cross = lax.ppermute(own, ALL, cross_pairs)  5.66 us
    dot_general x1, matrix products, body(): jnp.einsum('ljpq,ljrq->lrp', near_blocks, near_rows, preferred_element_ty...  4.6 us
    ppermute x1, starting transfers between devices, body(): lax.ppermute(jnp.take(everything, asked, axis=0), PAIR, [(0, 1), (1, 0)])  2.71 us
    broadcast_in_dim x4, local copies, waits for them, and re-layouts, body(): spread = jnp.broadcast_to(everything[None], (n,) + everything.shape)  1.6 us
    dot_general x1, matrix products, body(): jnp.einsum('lrp,lkp->lrk', density, basis, preferred_element_type=jnp.flo...  1.56 us
    dot_general x1, matrix products, body(): jnp.einsum('lkq,lrq->lrk', leaf_coupling, side_by_side(far_skels), prefer...  1.3 us
    gather x2, local copies, waits for them, and re-layouts, body(): jnp.take(skeleton_padded, halo_row(far_leaf), axis=0)  1.22 us
  transfers between devices with their start and end apart: 5, of which 2 were waited for; matrix products, arithmetic and copies ran while one was open for 33% of the time, Pallas kernels for 0%

profile of v1, /device:TPU:1, one launch (start us, length us, event | category | flops | bytes accessed | tf_op | source)
XLA Modules:
  0.0 43.6 jit_solution(2355332595567026922)
XLA Ops:
  0.0 1.6 %convolution_convert_fusion = bf16[32,8,64]{2,1,0:T(8,128)(2,1)S(1)} fusion(bf16[32,8,128]{2,1,0:T(8,128)(2,1)} %param.11, bf16[32,64,128]{2,1,0:T(8,128)(2,1)} %param.12), kind=kOutput, calls=%fused_computation.7 | convolution fusion | flops 4210688 | bytes 622592 | tf_op jit(solution)/shard_map/lrp,lkp->lrk/dot_general | solution.py:34
  1.7 1.1 %convolution_convert_fusion.2 = bf16[4,8,64]{2,1,0:T(8,128)(2,1)S(1)} fusion(bf16[4,8,512]{2,1,0:T(8,128)(2,1)S(1)} %reshape.82, bf16[4,64,512]{2,1,0:T(8,128)(2,1)} %param.17), kind=kOutput, calls=%fused_computation.9 | convolution fusion | flops 2099200 | bytes 299008 | tf_op jit(solution)/shard_map/ckq,crq->crk/dot_general | solution.py:38
  2.9 0.6 %broadcast_in_dim.57 = bf16[8,4,512]{2,1,0:T(4,128)(2,1)} broadcast(bf16[4,512]{1,0:T(4,128)(2,1)S(1)} %broadcast_in_dim.56), dimensions={1,2} | broadcast | bytes 36864 | tf_op jit(solution)/shard_map/broadcast_in_dim | solution.py:45
  3.6 9.0 %all-to-all-start = ((bf16[8,4,512]{2,1,0:T(4,128)(2,1)}), bf16[8,4,512]{2,1,0:T(4,128)(2,1)S(1)}, u32[]{:S(2)}, u32[]{:S(2)}) async-start(bf16[8,4,512]{2,1,0:T(4,128)(2,1)} %broadcast_in_dim.57), calls=%async_computation | async-start | bytes 65536 | tf_op jit(solution)/shard_map/all_to_all | solution.py:46
  12.7 0.8 %bitcast_dynamic-update-slice_fusion = bf16[32,1536]{1,0:T(8,128)(2,1)S(1)} fusion(bf16[4,8,8,128]{3,2,1,0:T(8,128)(2,1)} %bitcast.53), kind=kLoop, calls=%fused_computation.23 | loop fusion | bytes 131072
  13.6 5.7 %collective-permute-start.1 = (bf16[32,1536]{1,0:T(8,128)(2,1)S(1)}, bf16[32,1536]{1,0:T(8,128)(2,1)S(1)}, u32[]{:S(2)}, u32[]{:S(2)}) collective-permute-start(bf16[32,1536]{1,0:T(8,128)(2,1)S(1)} %constant_dynamic-update-slice_fusion), channel_id=1, source_target_pairs={{1,2},{3,4},{5,6},{7,8},{9,10},{11,12},{13,14},{15,16},{17,18},{19... | collective-permute-start | bytes 294920 | tf_op jit(solution)/shard_map/ppermute | solution.py:61
  19.2 0.7 %fusion.48 = (bf16[1,4,8]{2,1,0:T(4,128)(2,1)S(1)}, bf16[1,4,8]{2,1,0:T(4,128)(2,1)S(1)}) fusion(s32[4,8]{1,0:T(4,128)} %param.18), kind=kLoop, calls=%fused_computation.152 | loop fusion | flops 672 | bytes 256 | tf_op jit(solution)/shard_map/stack | solution.py:57
  20.1 0.7 %compare_and_fusion.2 = (pred[4,8]{1,0:T(4,128)(4,1)S(1)}, s32[4,8]{1,0:T(4,128)S(1)}, pred[4,8]{1,0:T(4,128)(4,1)S(1)}) fusion(s32[4,8]{1,0:T(4,128)} %param.18, s32[]{:T(128)S(6)} %axis_index.60), kind=kLoop, calls=%fused_computation.143 | loop fusion | flops 3872 | bytes 324 | tf_op jit(solution)/shard_map/jit(_take)/and | solution.py:108
  21.0 0.7 %compare_and_fusion = (pred[32,6]{0,1:T(8,128)(4,1)S(1)}, s32[32,6]{0,1:T(8,128)S(1)}, pred[32,6]{0,1:T(8,128)(4,1)S(1)}, s32[32,6]{0,1:T(8,128)S(1)}) fusion(pred[]{:T(512)S(6)} %eq.16, s32[32,6]{0,1:T(8,128)} %param.15, s32[]{:T(128)S(6)} %mul.49, s32[32,6]{0,1:T(8,128)} %param.13), kind=kLoop, calls=%fused_computation.40 | loop fusion | flops 6144 | bytes 3461 | tf_op jit(solution)/shard_map/jit(_take)/and | solution.py:84
  22.4 0.8 %broadcast_in_dim.59 = bf16[16,32,512]{2,1,0:T(8,128)(2,1)} broadcast(bf16[32,512]{1,0:T(8,128)(2,1)S(1)} %broadcast_in_dim.58), dimensions={1,2} | broadcast | bytes 557056 | tf_op jit(solution)/shard_map/broadcast_in_dim | solution.py:45
  23.2 4.7 %all-to-all-start.1 = ((bf16[16,32,512]{2,1,0:T(8,128)(2,1)}), bf16[16,32,512]{2,1,0:T(8,128)(2,1)S(1)}, u32[]{:S(2)}, u32[]{:S(2)}) async-start(bf16[16,32,512]{2,1,0:T(8,128)(2,1)} %broadcast_in_dim.59), calls=%async_computation.1 | async-start | bytes 1048576 | tf_op jit(solution)/shard_map/all_to_all | solution.py:46
  28.3 1.0 %gather_fusion.1 = bf16[192,512]{1,0:T(8,128)(2,1)S(1)} fusion(bf16[96,512]{1,0:T(8,128)(2,1)S(1)} %pad_maximum_fusion.1, s32[1024]{0:T(1024)S(1)} %pad_clamp_fusion.2), kind=kCustom, calls=%fused_computation.3 | custom fusion | bytes 393984 | tf_op jit(solution)/shard_map/jit(_take)/gather | solution.py:84
  29.3 0.2 gather.18
  29.7 0.3 reshape.86
  30.0 1.3 %fusion.50 = f32[32,8,64]{2,1,0:T(8,128)} fusion(bf16[32,8,384]{2,1,0:T(8,128)(2,1)S(1)} %reshape.86, bf16[32,64,384]{2,1,0:T(8,128)(2,1)S(1)} %copy-done), kind=kOutput, calls=%fused_computation.156 | convolution fusion | flops 12582912 | bytes 1835008 | tf_op jit(solution)/shard_map/lkq,lrq->lrk/dot_general | solution.py:87
  31.4 1.0 %gather_fusion = bf16[192,1024]{1,0:T(8,128)(2,1)S(1)} fusion(bf16[96,1024]{1,0:T(8,128)(2,1)S(1)} %slice.39, s32[1024]{0:T(1024)S(1)} %pad_clamp_fusion.3), kind=kCustom, calls=%fused_computation.2 | custom fusion | bytes 787200 | tf_op jit(solution)/shard_map/jit(_take)/gather | solution.py:78
  32.5 4.6 %convolution_bitcast_fusion = f32[32,8,128]{2,1,0:T(8,128)S(1)} fusion(bf16[32,6,128,128]{3,2,1,0:T(8,128)(2,1)} %param.14, bf16[32,6,8,128]{3,2,1,0:T(8,128)(2,1)S(1)} %bitcast.51, pred[32,6]{1,0:T(8,128)(4,1)S(1)} %copy.23), kind=kOutput, calls=%fused_computation.5 | convolution fusion | flops 50528256 | bytes 6815936 | tf_op jit(solution)/shard_map/ljpq,ljrq->lrp/dot_general | solution.py:81
  37.1 0.5 %all-to-all-done.1 = bf16[16,32,512]{2,1,0:T(8,128)(2,1)S(1)} async-done(((bf16[16,32,512]{2,1,0:T(8,128)(2,1)}), bf16[16,32,512]{2,1,0:T(8,128)(2,1)S(1)}, u32[]{:S(2)}, u32[]{:S(2)}) %all-to-all-start.1) | async-done | bytes 524320 | tf_op jit(solution)/shard_map/all_to_all | solution.py:46
  37.6 0.6 %gather_fusion.2 = bf16[32,512]{1,0:T(8,128)(2,1)S(1)} fusion(bf16[512,512]{1,0:T(8,128)(2,1)S(1)} %bitcast.49, s32[1024]{0:T(1024)S(1)} %pad_clamp_fusion.1), kind=kCustom, calls=%fused_computation.clone | custom fusion | bytes 65664 | tf_op jit(solution)/shard_map/jit(_take)/gather | solution.py:106
  38.3 2.7 %collective-permute-start.2 = (bf16[4,8,512]{2,1,0:T(8,128)(2,1)S(1)}, bf16[4,8,512]{2,1,0:T(8,128)(2,1)S(1)}, u32[]{:S(2)}, u32[]{:S(2)}) collective-permute-start(bf16[4,8,512]{2,1,0:T(8,128)(2,1)S(1)} %bitcast_select_fusion.1), channel_id=1, source_target_pairs={{0,1},{1,0},{2,3},{3,2},{4,5},{5,4},{6,7},{7,6},{8,9},{9,8},{10,11... | collective-permute-start | bytes 98312 | tf_op jit(solution)/shard_map/ppermute | solution.py:106
  41.1 0.6 %gather_fusion.3 = bf16[32,512]{1,0:T(8,128)(2,1)S(1)} fusion(bf16[512,512]{1,0:T(8,128)(2,1)S(1)} %bitcast.50, s32[1024]{0:T(1024)S(1)} %pad_clamp_fusion), kind=kCustom, calls=%fused_computation.1.clone | custom fusion | bytes 65664 | tf_op jit(solution)/shard_map/jit(_take)/gather | solution.py:108
  41.7 0.2 collective-permute-done.2
  42.3 0.3 fusion.1
  42.7 0.9 %fusion = bf16[32,8,128]{2,1,0:T(8,128)(2,1)} fusion(f32[32,8,128]{2,1,0:T(8,128)S(1)} %convolution_bitcast_fusion, bf16[32,8,64]{2,1,0:T(8,128)(2,1)S(1)} %fusion.7, bf16[32,64,128]{2,1,0:T(8,128)(2,1)S(1)} %copy-done.1), kind=kOutput, calls=%fused_computation.6 | convolution fusion | flops 4259840 | bytes 753664 | tf_op jit(solution)/shard_map/lrk,lkp->lrp/dot_general | solution.py:123
  (53 shorter events, 2.4 us)
Async XLA Ops:
  0.0 30.0 %copy-start = (bf16[32,64,384]{2,1,0:T(8,128)(2,1)S(1)}, bf16[32,64,384]{2,1,0:T(8,128)(2,1)}, u32[]{:S(2)}) copy-start(bf16[32,64,384]{2,1,0:T(8,128)(2,1)} %param.16) | copy-start | bytes 4718596
  3.6 18.8 %all-to-all-start = ((bf16[8,4,512]{2,1,0:T(4,128)(2,1)}), bf16[8,4,512]{2,1,0:T(4,128)(2,1)S(1)}, u32[]{:S(2)}, u32[]{:S(2)}) async-start(bf16[8,4,512]{2,1,0:T(4,128)(2,1)} %broadcast_in_dim.57), calls=%async_computation | async-start | bytes 65536 | tf_op jit(solution)/shard_map/all_to_all | solution.py:46
  13.6 14.7 %collective-permute-start.1 = (bf16[32,1536]{1,0:T(8,128)(2,1)S(1)}, bf16[32,1536]{1,0:T(8,128)(2,1)S(1)}, u32[]{:S(2)}, u32[]{:S(2)}) collective-permute-start(bf16[32,1536]{1,0:T(8,128)(2,1)S(1)} %constant_dynamic-update-slice_fusion), channel_id=1, source_target_pairs={{1,2},{3,4},{5,6},{7,8},{9,10},{11,12},{13,14},{15,16},{17,18},{19... | collective-permute-start | bytes 294920 | tf_op jit(solution)/shard_map/ppermute | solution.py:61
  20.0 7.9 %collective-permute-start = (bf16[33,1536]{1,0:T(8,128)(2,1)S(1)}, bf16[33,1536]{1,0:T(8,128)(2,1)S(1)}, u32[]{:S(2)}, u32[]{:S(2)}) collective-permute-start(bf16[33,1536]{1,0:T(8,128)(2,1)S(1)} %fusion.8), channel_id=1, source_target_pairs={{0,1},{1,0},{2,3},{3,2},{4,5},{5,4},{6,7},{7,6},{8,9},{9,8},{10,11... | collective-permute-start | bytes 304136 | tf_op jit(solution)/shard_map/ppermute | solution.py:62
  23.2 14.4 %all-to-all-start.1 = ((bf16[16,32,512]{2,1,0:T(8,128)(2,1)}), bf16[16,32,512]{2,1,0:T(8,128)(2,1)S(1)}, u32[]{:S(2)}, u32[]{:S(2)}) async-start(bf16[16,32,512]{2,1,0:T(8,128)(2,1)} %broadcast_in_dim.59), calls=%async_computation.1 | async-start | bytes 1048576 | tf_op jit(solution)/shard_map/all_to_all | solution.py:46
  31.4 10.9 %copy-start.2 = (bf16[4,64,512]{2,1,0:T(8,128)(2,1)S(1)}, bf16[4,64,512]{2,1,0:T(8,128)(2,1)}, u32[]{:S(2)}) copy-start(bf16[4,64,512]{2,1,0:T(8,128)(2,1)} %param.17) | copy-start | bytes 786436
  31.4 11.4 %copy-start.1 = (bf16[32,64,128]{2,1,0:T(8,128)(2,1)S(1)}, bf16[32,64,128]{2,1,0:T(8,128)(2,1)}, u32[]{:S(2)}) copy-start(bf16[32,64,128]{2,1,0:T(8,128)(2,1)} %param.12) | copy-start | bytes 1572868
  32.5 9.8 %copy-start.4 = (bf16[4,64,512]{2,1,0:T(8,128)(2,1)S(1)}, bf16[4,64,512]{2,1,0:T(8,128)(2,1)}, u32[]{:S(2)}) copy-start(bf16[4,64,512]{2,1,0:T(8,128)(2,1)} %param.19) | copy-start | bytes 786436
  32.5 10.2 %copy-start.3 = (f32[32,8,64]{2,1,0:T(8,128)S(1)}, f32[32,8,64]{2,1,0:T(8,128)}, u32[]{:S(2)}) copy-start(f32[32,8,64]{2,1,0:T(8,128)} %fusion.50) | copy-start | bytes 196612
  38.3 3.6 %collective-permute-start.2 = (bf16[4,8,512]{2,1,0:T(8,128)(2,1)S(1)}, bf16[4,8,512]{2,1,0:T(8,128)(2,1)S(1)}, u32[]{:S(2)}, u32[]{:S(2)}) collective-permute-start(bf16[4,8,512]{2,1,0:T(8,128)(2,1)S(1)} %bitcast_select_fusion.1), channel_id=1, source_target_pairs={{0,1},{1,0},{2,3},{3,2},{4,5},{5,4},{6,7},{7,6},{8,9},{9,8},{10,11... | collective-permute-start | bytes 98312 | tf_op jit(solution)/shard_map/ppermute | solution.py:106

commit v2 on v1

--- a/solution.py
+++ b/solution.py
@@ -75,13 +75,13 @@
         high = jnp.where(even, t - leaf_count, t + leaf_count)
         return jnp.where(t < 0, low, jnp.where(t < leaf_count, t + leaf_count, high))
 
-    near_rows = jnp.take(density_padded, halo_row(near_list), axis=0).reshape(
+    near_rows = jnp.take(density_padded, halo_row(near_list), axis=0, mode="clip").reshape(
         leaf_count, near_list.shape[1], rhs_count, leaf_width
     )
     near_part = jnp.einsum(
         "ljpq,ljrq->lrp", near_blocks, near_rows, preferred_element_type=jnp.float32
     )
-    far_skels = jnp.take(skeleton_padded, halo_row(far_leaf), axis=0).reshape(
+    far_skels = jnp.take(skeleton_padded, halo_row(far_leaf), axis=0, mode="clip").reshape(
         leaf_count, far_count, rhs_count, rank_width
     )
     leaf_far = jnp.einsum(
@@ -103,9 +103,9 @@
 
     row, elsewhere = placed(far_coarse)
     asked, _ = placed(partner_far)
-    served = lax.ppermute(jnp.take(everything, asked, axis=0), PAIR, [(0, 1), (1, 0)])
+    served = lax.ppermute(jnp.take(everything, asked, axis=0, mode="clip"), PAIR, [(0, 1), (1, 0)])
     coarse_skels = jnp.where(
-        elsewhere[:, :, None], served, jnp.take(everything, row, axis=0)
+        elsewhere[:, :, None], served, jnp.take(everything, row, axis=0, mode="clip")
     ).reshape(box_count, coarse_count, rhs_count, rank_width)
     coarse_field = jnp.einsum(
         "ckq,crq->crk", coarse_coupling, side_by_side(coarse_skels), preferred_element_type=jnp.float32

time: 44 us -> 43.8 us (level)
    and x3 -> x0, other arithmetic: 1.52 us -> none  [the longest x1 0.74 us: body(): jnp.take(everything, row, axis=0)]
    add x0 -> x2, other arithmetic: none -> 0.79 us  [placed(): return (position * box_count + slot, coords[PAIR] != lax.axis_index(PAIR))]
    ne x0 -> x1, other arithmetic: none -> 0.7 us  [placed(): return (position * box_count + slot, coords[PAIR] != lax.axis_index(PAIR))]
    another operation x2 -> x1, other arithmetic: 0.71 us -> 0.01 us  [body(): jnp.stack([far_coarse // 32, far_coarse % 32]).reshape(1, -1)]
    select_n x2, other arithmetic: 0.15 us -> 0.79 us  [the longest x1 0.71 us: halo_row(): jnp.where(t < 0, low, jnp.where(t < leaf_count, t + leaf_count, high))]
    gather x5 -> x4, local copies, waits for them, and re-layouts: 3.49 us -> 3.27 us  [the longest x1 1.02 us: body(): jnp.take(density_padded, halo_row(near_list), axis=0, mode='clip')]
where the time goes in v2:
time: 43.8 us; the launch traced here: 43.4 us
  starting transfers between devices  22.5 us (51%)
  matrix products  9.68 us (22%)
  local copies, waits for them, and re-layouts  7.83 us (18%)
  other arithmetic  2.46 us (6%)
  waiting for transfers between devices  0.53 us (1%)
    all_to_all x2, starting transfers between devices, body(): moved = lax.all_to_all(spread, axes, 0, 0, tiled=False)  13.7 us
    ppermute x1, starting transfers between devices, body(): cross = lax.ppermute(own, ALL, cross_pairs)  5.66 us
    dot_general x1, matrix products, body(): jnp.einsum('ljpq,ljrq->lrp', near_blocks, near_rows, preferred_element_ty...  4.55 us
    ppermute x1, starting transfers between devices, body(): lax.ppermute(jnp.take(everything, asked, axis=0, mode='clip'), PAIR, [(0,...  3.06 us
    broadcast_in_dim x4, local copies, waits for them, and re-layouts, body(): spread = jnp.broadcast_to(everything[None], (n,) + everything.shape)  1.59 us
    dot_general x1, matrix products, body(): jnp.einsum('lrp,lkp->lrk', density, basis, preferred_element_type=jnp.flo...  1.56 us
    dot_general x1, matrix products, body(): jnp.einsum('lkq,lrq->lrk', leaf_coupling, side_by_side(far_skels), prefer...  1.3 us
    dot_general x1, matrix products, body(): jnp.einsum('ckq,crq->crk', transfer, side_by_side(children), preferred_el...  1.11 us
  transfers between devices with their start and end apart: 5, of which 2 were waited for; matrix products, arithmetic and copies ran while one was open for 33% of the time, Pallas kernels for 0%

profile of v2, /device:TPU:1, one launch (start us, length us, event | category | flops | bytes accessed | tf_op | source)
XLA Modules:
  0.0 43.4 jit_solution(14119337470920592311)
XLA Ops:
  0.0 1.6 %convolution_convert_fusion = bf16[32,8,64]{2,1,0:T(8,128)(2,1)S(1)} fusion(bf16[32,8,128]{2,1,0:T(8,128)(2,1)} %param.9, bf16[32,64,128]{2,1,0:T(8,128)(2,1)} %param.10), kind=kOutput, calls=%fused_computation.7 | convolution fusion | flops 4210688 | bytes 622592 | tf_op jit(solution)/shard_map/lrp,lkp->lrk/dot_general | solution.py:34
  1.7 1.1 %convolution_convert_fusion.2 = bf16[4,8,64]{2,1,0:T(8,128)(2,1)S(1)} fusion(bf16[4,8,512]{2,1,0:T(8,128)(2,1)S(1)} %reshape.69, bf16[4,64,512]{2,1,0:T(8,128)(2,1)} %param.15), kind=kOutput, calls=%fused_computation.9 | convolution fusion | flops 2099200 | bytes 299008 | tf_op jit(solution)/shard_map/ckq,crq->crk/dot_general | solution.py:38
  2.9 0.6 %broadcast_in_dim.39 = bf16[8,4,512]{2,1,0:T(4,128)(2,1)} broadcast(bf16[4,512]{1,0:T(4,128)(2,1)S(1)} %broadcast_in_dim.38), dimensions={1,2} | broadcast | bytes 36864 | tf_op jit(solution)/shard_map/broadcast_in_dim | solution.py:45
  3.6 9.0 %all-to-all-start = ((bf16[8,4,512]{2,1,0:T(4,128)(2,1)}), bf16[8,4,512]{2,1,0:T(4,128)(2,1)S(1)}, u32[]{:S(2)}, u32[]{:S(2)}) async-start(bf16[8,4,512]{2,1,0:T(4,128)(2,1)} %broadcast_in_dim.39), calls=%async_computation | async-start | bytes 65536 | tf_op jit(solution)/shard_map/all_to_all | solution.py:46
  12.7 0.8 %bitcast_dynamic-update-slice_fusion = bf16[32,1536]{1,0:T(8,128)(2,1)S(1)} fusion(bf16[4,8,8,128]{3,2,1,0:T(8,128)(2,1)} %bitcast.53), kind=kLoop, calls=%fused_computation.19 | loop fusion | bytes 131072
  13.6 5.7 %collective-permute-start.1 = (bf16[32,1536]{1,0:T(8,128)(2,1)S(1)}, bf16[32,1536]{1,0:T(8,128)(2,1)S(1)}, u32[]{:S(2)}, u32[]{:S(2)}) collective-permute-start(bf16[32,1536]{1,0:T(8,128)(2,1)S(1)} %constant_dynamic-update-slice_fusion), channel_id=1, source_target_pairs={{1,2},{3,4},{5,6},{7,8},{9,10},{11,12},{13,14},{15,16},{17,18},{19... | collective-permute-start | bytes 294920 | tf_op jit(solution)/shard_map/ppermute | solution.py:61
  19.2 0.7 %fusion.27 = (s32[4,8]{1,0:T(4,128)S(1)}, bf16[1,4,8]{2,1,0:T(4,128)(2,1)S(1)}, bf16[1,4,8]{2,1,0:T(4,128)(2,1)S(1)}) fusion(s32[4,8]{1,0:T(4,128)} %param.16), kind=kLoop, calls=%fused_computation.109 | loop fusion | flops 4032 | bytes 384 | tf_op jit(solution)/shard_map/add | solution.py:102
  20.2 0.7 %fusion.9 = pred[4,8]{1,0:T(4,128)(4,1)S(1)} fusion(s32[]{:T(128)S(6)} %axis_index.60, s32[4,8]{1,0:T(4,128)} %param.16), kind=kLoop, calls=%fused_computation.91 | loop fusion | flops 864 | bytes 164 | tf_op jit(solution)/shard_map/ne | solution.py:102
  21.0 0.7 %fusion.5 = (s32[32,6]{0,1:T(8,128)S(1)}, s32[32,6]{0,1:T(8,128)S(1)}) fusion(s32[32,6]{0,1:T(8,128)} %param.11, s32[]{:T(128)S(6)} %mul.49, pred[]{:T(512)S(6)} %eq.16, s32[32,6]{0,1:T(8,128)} %param.13), kind=kLoop, calls=%fused_computation.23 | loop fusion | flops 3840 | bytes 3077 | tf_op jit(solution)/shard_map/jit(_where)/select_n | solution.py:76
  22.1 0.8 %broadcast_in_dim.41 = bf16[16,32,512]{2,1,0:T(8,128)(2,1)} broadcast(bf16[32,512]{1,0:T(8,128)(2,1)S(1)} %broadcast_in_dim.40), dimensions={1,2} | broadcast | bytes 557056 | tf_op jit(solution)/shard_map/broadcast_in_dim | solution.py:45
  23.0 4.7 %all-to-all-start.1 = ((bf16[16,32,512]{2,1,0:T(8,128)(2,1)}), bf16[16,32,512]{2,1,0:T(8,128)(2,1)S(1)}, u32[]{:S(2)}, u32[]{:S(2)}) async-start(bf16[16,32,512]{2,1,0:T(8,128)(2,1)} %broadcast_in_dim.41), calls=%async_computation.1 | async-start | bytes 1048576 | tf_op jit(solution)/shard_map/all_to_all | solution.py:46
  28.1 1.0 %gather_fusion.1 = bf16[192,512]{1,0:T(8,128)(2,1)S(1)} fusion(bf16[96,512]{1,0:T(8,128)(2,1)S(1)} %pad_maximum_fusion.1, s32[1024]{0:T(1024)S(1)} %pad_clamp_fusion.2), kind=kCustom, calls=%fused_computation.1 | custom fusion | bytes 393984 | tf_op jit(solution)/shard_map/jit(_take)/gather | solution.py:84
  29.1 0.2 reshape.74
  29.4 0.3 reshape.75
  29.8 1.3 %fusion.44 = f32[32,8,64]{2,1,0:T(8,128)} fusion(bf16[32,8,384]{2,1,0:T(8,128)(2,1)S(1)} %reshape.75, bf16[32,64,384]{2,1,0:T(8,128)(2,1)S(1)} %copy-done), kind=kOutput, calls=%fused_computation.141 | convolution fusion | flops 12582912 | bytes 1835008 | tf_op jit(solution)/shard_map/lkq,lrq->lrk/dot_general | solution.py:87
  31.2 1.0 %gather_fusion = bf16[192,1024]{1,0:T(8,128)(2,1)S(1)} fusion(bf16[96,1024]{1,0:T(8,128)(2,1)S(1)} %slice.39, s32[1024]{0:T(1024)S(1)} %pad_clamp_fusion.3), kind=kCustom, calls=%fused_computation | custom fusion | bytes 787200 | tf_op jit(solution)/shard_map/jit(_take)/gather | solution.py:78
  32.3 4.5 %convolution_bitcast_fusion = f32[32,8,128]{2,1,0:T(8,128)S(1)} fusion(bf16[32,6,8,128]{3,2,1,0:T(8,128)(2,1)S(1)} %bitcast.51, bf16[32,6,128,128]{3,2,1,0:T(8,128)(2,1)} %param.12), kind=kOutput, calls=%fused_computation.5 | convolution fusion | flops 50331648 | bytes 6815744 | tf_op jit(solution)/shard_map/ljpq,ljrq->lrp/dot_general | solution.py:81
  36.8 0.3 all-to-all-done.1
  37.1 0.6 %gather_fusion.2 = bf16[32,512]{1,0:T(8,128)(2,1)S(1)} fusion(bf16[512,512]{1,0:T(8,128)(2,1)S(1)} %bitcast.49, s32[1024]{0:T(1024)S(1)} %pad_clamp_fusion.1), kind=kCustom, calls=%fused_computation.2 | custom fusion | bytes 65664 | tf_op jit(solution)/shard_map/jit(_take)/gather | solution.py:106
  37.8 3.1 %collective-permute-start.2 = (bf16[4,8,512]{2,1,0:T(8,128)(2,1)S(1)}, bf16[4,8,512]{2,1,0:T(8,128)(2,1)S(1)}, u32[]{:S(2)}, u32[]{:S(2)}) collective-permute-start(bf16[4,8,512]{2,1,0:T(8,128)(2,1)S(1)} %bitcast.55), channel_id=1, source_target_pairs={{0,1},{1,0},{2,3},{3,2},{4,5},{5,4},{6,7},{7,6},{8,9},{9,8},{10,11... | collective-permute-start | bytes 98312 | tf_op jit(solution)/shard_map/ppermute | solution.py:106
  40.8 0.6 %gather_fusion.3 = bf16[32,512]{1,0:T(8,128)(2,1)S(1)} fusion(bf16[512,512]{1,0:T(8,128)(2,1)S(1)} %bitcast.50, s32[1024]{0:T(1024)S(1)} %pad_clamp_fusion), kind=kCustom, calls=%fused_computation.3 | custom fusion | bytes 65664 | tf_op jit(solution)/shard_map/jit(_take)/gather | solution.py:108
  41.4 0.2 collective-permute-done.2
  42.0 0.3 fusion.1
  42.5 0.9 %fusion = bf16[32,8,128]{2,1,0:T(8,128)(2,1)} fusion(f32[32,8,128]{2,1,0:T(8,128)S(1)} %convolution_bitcast_fusion, bf16[32,8,64]{2,1,0:T(8,128)(2,1)S(1)} %fusion.3, bf16[32,64,128]{2,1,0:T(8,128)(2,1)S(1)} %copy-done.1), kind=kOutput, calls=%fused_computation.6 | convolution fusion | flops 4259840 | bytes 753664 | tf_op jit(solution)/shard_map/lrk,lkp->lrp/dot_general | solution.py:123
  (50 shorter events, 2.1 us)
Async XLA Ops:
  0.0 29.8 %copy-start = (bf16[32,64,384]{2,1,0:T(8,128)(2,1)S(1)}, bf16[32,64,384]{2,1,0:T(8,128)(2,1)}, u32[]{:S(2)}) copy-start(bf16[32,64,384]{2,1,0:T(8,128)(2,1)} %param.14) | copy-start | bytes 4718596
  3.6 18.6 %all-to-all-start = ((bf16[8,4,512]{2,1,0:T(4,128)(2,1)}), bf16[8,4,512]{2,1,0:T(4,128)(2,1)S(1)}, u32[]{:S(2)}, u32[]{:S(2)}) async-start(bf16[8,4,512]{2,1,0:T(4,128)(2,1)} %broadcast_in_dim.39), calls=%async_computation | async-start | bytes 65536 | tf_op jit(solution)/shard_map/all_to_all | solution.py:46
  13.6 14.5 %collective-permute-start.1 = (bf16[32,1536]{1,0:T(8,128)(2,1)S(1)}, bf16[32,1536]{1,0:T(8,128)(2,1)S(1)}, u32[]{:S(2)}, u32[]{:S(2)}) collective-permute-start(bf16[32,1536]{1,0:T(8,128)(2,1)S(1)} %constant_dynamic-update-slice_fusion), channel_id=1, source_target_pairs={{1,2},{3,4},{5,6},{7,8},{9,10},{11,12},{13,14},{15,16},{17,18},{19... | collective-permute-start | bytes 294920 | tf_op jit(solution)/shard_map/ppermute | solution.py:61
  20.1 7.6 %collective-permute-start = (bf16[33,1536]{1,0:T(8,128)(2,1)S(1)}, bf16[33,1536]{1,0:T(8,128)(2,1)S(1)}, u32[]{:S(2)}, u32[]{:S(2)}) collective-permute-start(bf16[33,1536]{1,0:T(8,128)(2,1)S(1)} %fusion.4), channel_id=1, source_target_pairs={{0,1},{1,0},{2,3},{3,2},{4,5},{5,4},{6,7},{7,6},{8,9},{9,8},{10,11... | collective-permute-start | bytes 304136 | tf_op jit(solution)/shard_map/ppermute | solution.py:62
  23.0 14.1 %all-to-all-start.1 = ((bf16[16,32,512]{2,1,0:T(8,128)(2,1)}), bf16[16,32,512]{2,1,0:T(8,128)(2,1)S(1)}, u32[]{:S(2)}, u32[]{:S(2)}) async-start(bf16[16,32,512]{2,1,0:T(8,128)(2,1)} %broadcast_in_dim.41), calls=%async_computation.1 | async-start | bytes 1048576 | tf_op jit(solution)/shard_map/all_to_all | solution.py:46
  31.1 10.8 %copy-start.2 = (bf16[4,64,512]{2,1,0:T(8,128)(2,1)S(1)}, bf16[4,64,512]{2,1,0:T(8,128)(2,1)}, u32[]{:S(2)}) copy-start(bf16[4,64,512]{2,1,0:T(8,128)(2,1)} %param.15) | copy-start | bytes 786436
  31.2 11.3 %copy-start.1 = (bf16[32,64,128]{2,1,0:T(8,128)(2,1)S(1)}, bf16[32,64,128]{2,1,0:T(8,128)(2,1)}, u32[]{:S(2)}) copy-start(bf16[32,64,128]{2,1,0:T(8,128)(2,1)} %param.10) | copy-start | bytes 1572868
  32.3 9.7 %copy-start.4 = (bf16[4,64,512]{2,1,0:T(8,128)(2,1)S(1)}, bf16[4,64,512]{2,1,0:T(8,128)(2,1)}, u32[]{:S(2)}) copy-start(bf16[4,64,512]{2,1,0:T(8,128)(2,1)} %param.17) | copy-start | bytes 786436
  32.3 10.2 %copy-start.3 = (f32[32,8,64]{2,1,0:T(8,128)S(1)}, f32[32,8,64]{2,1,0:T(8,128)}, u32[]{:S(2)}) copy-start(f32[32,8,64]{2,1,0:T(8,128)} %fusion.44) | copy-start | bytes 196612
  37.8 3.9 %collective-permute-start.2 = (bf16[4,8,512]{2,1,0:T(8,128)(2,1)S(1)}, bf16[4,8,512]{2,1,0:T(8,128)(2,1)S(1)}, u32[]{:S(2)}, u32[]{:S(2)}) collective-permute-start(bf16[4,8,512]{2,1,0:T(8,128)(2,1)S(1)} %bitcast.55), channel_id=1, source_target_pairs={{0,1},{1,0},{2,3},{3,2},{4,5},{5,4},{6,7},{7,6},{8,9},{9,8},{10,11... | collective-permute-start | bytes 98312 | tf_op jit(solution)/shard_map/ppermute | solution.py:106

commit v3 on v2

--- a/solution.py
+++ b/solution.py
@@ -42,11 +42,12 @@
     everything = coarse_flat
     for axes in STAGES:
         n = lax.axis_size(axes)
-        spread = jnp.broadcast_to(everything[None], (n,) + everything.shape)
-        moved = lax.all_to_all(spread, axes, 0, 0, tiled=False)
-        everything = moved.reshape(
-            (n * everything.shape[0],) + everything.shape[1:]
-        )
+        if len(axes) == 1:
+            everything = lax.all_gather(everything, axes, axis=0, tiled=True)
+        else:
+            spread = jnp.broadcast_to(everything[None], (n,) + everything.shape)
+            moved = lax.all_to_all(spread, axes, 0, 0, tiled=False)
+            everything = moved.reshape((n * everything.shape[0],) + everything.shape[1:])
     density_flat = density.reshape(leaf_count, rhs_count * leaf_width)
     skeleton_flat = skeleton.reshape(leaf_count, rhs_count * rank_width)
     device_count = lax.axis_size(ALL)

time: 43.8 us -> 60.8 us (1.39)
  blocking collectives: 0 us -> 24.2 us
  starting transfers between devices: 22.5 us -> 16.3 us
  local copies, waits for them, and re-layouts: 7.83 us -> 7.22 us
    all_gather x0 -> x1, blocking collectives: none -> 24.2 us  [body(): everything = lax.all_gather(everything, axes, axis=0, tiled=True)]
    all_to_all x2 -> x1, starting transfers between devices: 13.7 us -> 3.57 us  [body(): moved = lax.all_to_all(spread, axes, 0, 0, tiled=False)]
    ppermute x1, starting transfers between devices: 3.06 us -> 6.47 us  [body(): lax.ppermute(jnp.take(everything, asked, axis=0, mode='clip'), PAIR, [(0,...]
    broadcast_in_dim x4 -> x1, local copies, waits for them, and re-layouts: 1.59 us -> 0.85 us  [body(): spread = jnp.broadcast_to(everything[None], (n,) + everything.shape)]
  transfers between devices with their start and end apart: 5 -> 4, of which waited for: 2 -> 1; matrix products, arithmetic and copies ran while one was open for 33% -> 24% of each run, Pallas kernels for 0% -> 0%
where the time goes in v3:
time: 60.8 us; the launch traced here: 60.5 us
  blocking collectives  24.2 us (40%)
  starting transfers between devices  16.3 us (27%)
  matrix products  9.68 us (16%)
  local copies, waits for them, and re-layouts  7.22 us (12%)
  other arithmetic  2.46 us (4%)
    all_gather x1, blocking collectives, body(): everything = lax.all_gather(everything, axes, axis=0, tiled=True)  24.2 us
    ppermute x1, starting transfers between devices, body(): lax.ppermute(jnp.take(everything, asked, axis=0, mode='clip'), PAIR, [(0,...  6.47 us
    ppermute x1, starting transfers between devices, body(): cross = lax.ppermute(own, ALL, cross_pairs)  6.2 us
    dot_general x1, matrix products, body(): jnp.einsum('ljpq,ljrq->lrp', near_blocks, near_rows, preferred_element_ty...  4.55 us
    all_to_all x1, starting transfers between devices, body(): moved = lax.all_to_all(spread, axes, 0, 0, tiled=False)  3.57 us
    dot_general x1, matrix products, body(): jnp.einsum('lrp,lkp->lrk', density, basis, preferred_element_type=jnp.flo...  1.56 us
    dot_general x1, matrix products, body(): jnp.einsum('lkq,lrq->lrk', leaf_coupling, side_by_side(far_skels), prefer...  1.3 us
  transfers between devices with their start and end apart: 4, of which 1 were waited for; matrix products, arithmetic and copies ran while one was open for 24% of the time, Pallas kernels for 0%

profile of v3, /device:TPU:1, one launch (start us, length us, event | category | flops | bytes accessed | tf_op | source)
XLA Modules:
  0.0 60.5 jit_solution(9577099449009274049)
XLA Ops:
  0.0 1.6 %convolution_convert_fusion = bf16[32,8,64]{2,1,0:T(8,128)(2,1)S(1)} fusion(bf16[32,8,128]{2,1,0:T(8,128)(2,1)} %param.9, bf16[32,64,128]{2,1,0:T(8,128)(2,1)} %param.10), kind=kOutput, calls=%fused_computation.7 | convolution fusion | flops 4210688 | bytes 622592 | tf_op jit(solution)/shard_map/lrp,lkp->lrk/dot_general | solution.py:34
  1.6 0.1 reshape.75
  1.7 0.9 %bitcast_dynamic-update-slice_fusion = bf16[32,1536]{1,0:T(8,128)(2,1)S(1)} fusion(bf16[4,8,8,128]{3,2,1,0:T(8,128)(2,1)} %bitcast.53), kind=kLoop, calls=%fused_computation.19 | loop fusion | bytes 131072
  2.6 6.2 %collective-permute-start.1 = (bf16[32,1536]{1,0:T(8,128)(2,1)S(1)}, bf16[32,1536]{1,0:T(8,128)(2,1)S(1)}, u32[]{:S(2)}, u32[]{:S(2)}) collective-permute-start(bf16[32,1536]{1,0:T(8,128)(2,1)S(1)} %constant_dynamic-update-slice_fusion), channel_id=1, source_target_pairs={{1,2},{3,4},{5,6},{7,8},{9,10},{11,12},{13,14},{15,16},{17,18},{19... | collective-permute-start | bytes 294920 | tf_op jit(solution)/shard_map/ppermute | solution.py:62
  8.8 0.7 %fusion.27 = (s32[4,8]{1,0:T(4,128)S(1)}, bf16[1,4,8]{2,1,0:T(4,128)(2,1)S(1)}, bf16[1,4,8]{2,1,0:T(4,128)(2,1)S(1)}) fusion(s32[4,8]{1,0:T(4,128)} %param.16), kind=kLoop, calls=%fused_computation.109 | loop fusion | flops 4032 | bytes 384 | tf_op jit(solution)/shard_map/add | solution.py:103
  9.9 1.1 %convolution_convert_fusion.2 = bf16[4,8,64]{2,1,0:T(8,128)(2,1)S(1)} fusion(bf16[4,8,512]{2,1,0:T(8,128)(2,1)S(1)} %reshape.71, bf16[4,64,512]{2,1,0:T(8,128)(2,1)} %param.15), kind=kOutput, calls=%fused_computation.9 | convolution fusion | flops 2099200 | bytes 299008 | tf_op jit(solution)/shard_map/ckq,crq->crk/dot_general | solution.py:38
  11.1 24.2 %all-gather = bf16[8,4,512]{2,1,0:T(4,128)(2,1)S(1)} all-gather(bf16[1,4,512]{2,1,0:T(4,128)(2,1)S(1)} %reshape.125), channel_id=1, replica_groups=mesh['z'=8,'x'=4,'y_lo'=2,'y_hi'=2,'core'=2] {'z'}, dimensions={0}, use_global_device_ids=true | all-gather | bytes 36864 | tf_op jit(solution)/shard_map/all_gather | solution.py:46
  35.3 0.9 %broadcast_in_dim.30 = bf16[16,32,512]{2,1,0:T(8,128)(2,1)} broadcast(bf16[32,512]{1,0:T(8,128)(2,1)S(1)} %reshape.126), dimensions={1,2} | broadcast | bytes 557056 | tf_op jit(solution)/shard_map/broadcast_in_dim | solution.py:48
  36.1 3.6 %all-to-all-start = ((bf16[16,32,512]{2,1,0:T(8,128)(2,1)}), bf16[16,32,512]{2,1,0:T(8,128)(2,1)S(1)}, u32[]{:S(2)}, u32[]{:S(2)}) async-start(bf16[16,32,512]{2,1,0:T(8,128)(2,1)} %broadcast_in_dim.30), calls=%async_computation | async-start | bytes 1048576 | tf_op jit(solution)/shard_map/all_to_all | solution.py:49
  39.7 0.7 %fusion.9 = pred[4,8]{1,0:T(4,128)(4,1)S(1)} fusion(s32[]{:T(128)S(6)} %axis_index.60, s32[4,8]{1,0:T(4,128)} %param.16), kind=kLoop, calls=%fused_computation.91 | loop fusion | flops 864 | bytes 164 | tf_op jit(solution)/shard_map/ne | solution.py:103
  40.5 0.7 %fusion.5 = (s32[32,6]{0,1:T(8,128)S(1)}, s32[32,6]{0,1:T(8,128)S(1)}) fusion(s32[32,6]{0,1:T(8,128)} %param.11, s32[]{:T(128)S(6)} %mul.49, pred[]{:T(512)S(6)} %eq.16, s32[32,6]{0,1:T(8,128)} %param.13), kind=kLoop, calls=%fused_computation.23 | loop fusion | flops 3840 | bytes 3077 | tf_op jit(solution)/shard_map/jit(_where)/select_n | solution.py:77
  42.0 1.0 %gather_fusion.1 = bf16[192,512]{1,0:T(8,128)(2,1)S(1)} fusion(bf16[96,512]{1,0:T(8,128)(2,1)S(1)} %pad_maximum_fusion.1, s32[1024]{0:T(1024)S(1)} %pad_clamp_fusion.2), kind=kCustom, calls=%fused_computation.1 | custom fusion | bytes 393984 | tf_op jit(solution)/shard_map/jit(_take)/gather | solution.py:85
  43.0 0.2 reshape.77
  43.3 0.1 copy.35
  43.4 0.3 reshape.78
  43.7 1.3 %fusion.44 = f32[32,8,64]{2,1,0:T(8,128)} fusion(bf16[32,8,384]{2,1,0:T(8,128)(2,1)S(1)} %reshape.78, bf16[32,64,384]{2,1,0:T(8,128)(2,1)S(1)} %copy-done), kind=kOutput, calls=%fused_computation.141 | convolution fusion | flops 12582912 | bytes 1835008 | tf_op jit(solution)/shard_map/lkq,lrq->lrk/dot_general | solution.py:88
  45.1 1.0 %gather_fusion = bf16[192,1024]{1,0:T(8,128)(2,1)S(1)} fusion(bf16[96,1024]{1,0:T(8,128)(2,1)S(1)} %slice.39, s32[1024]{0:T(1024)S(1)} %pad_clamp_fusion.3), kind=kCustom, calls=%fused_computation | custom fusion | bytes 787200 | tf_op jit(solution)/shard_map/jit(_take)/gather | solution.py:79
  46.2 4.5 %convolution_bitcast_fusion = f32[32,8,128]{2,1,0:T(8,128)S(1)} fusion(bf16[32,6,8,128]{3,2,1,0:T(8,128)(2,1)S(1)} %bitcast.51, bf16[32,6,128,128]{3,2,1,0:T(8,128)(2,1)} %param.12), kind=kOutput, calls=%fused_computation.5 | convolution fusion | flops 50331648 | bytes 6815744 | tf_op jit(solution)/shard_map/ljpq,ljrq->lrp/dot_general | solution.py:82
  50.8 0.6 %gather_fusion.2 = bf16[32,512]{1,0:T(8,128)(2,1)S(1)} fusion(bf16[512,512]{1,0:T(8,128)(2,1)S(1)} %bitcast.49, s32[1024]{0:T(1024)S(1)} %pad_clamp_fusion.1), kind=kCustom, calls=%fused_computation.2 | custom fusion | bytes 65664 | tf_op jit(solution)/shard_map/jit(_take)/gather | solution.py:107
  51.4 6.5 %collective-permute-start.2 = (bf16[4,8,512]{2,1,0:T(8,128)(2,1)S(1)}, bf16[4,8,512]{2,1,0:T(8,128)(2,1)S(1)}, u32[]{:S(2)}, u32[]{:S(2)}) collective-permute-start(bf16[4,8,512]{2,1,0:T(8,128)(2,1)S(1)} %bitcast.55), channel_id=1, source_target_pairs={{0,1},{1,0},{2,3},{3,2},{4,5},{5,4},{6,7},{7,6},{8,9},{9,8},{10,11... | collective-permute-start | bytes 98312 | tf_op jit(solution)/shard_map/ppermute | solution.py:107
  57.9 0.6 %gather_fusion.3 = bf16[32,512]{1,0:T(8,128)(2,1)S(1)} fusion(bf16[512,512]{1,0:T(8,128)(2,1)S(1)} %bitcast.50, s32[1024]{0:T(1024)S(1)} %pad_clamp_fusion), kind=kCustom, calls=%fused_computation.3 | custom fusion | bytes 65664 | tf_op jit(solution)/shard_map/jit(_take)/gather | solution.py:109
  58.5 0.2 collective-permute-done.2
  59.1 0.3 fusion.1
  59.6 0.9 %fusion = bf16[32,8,128]{2,1,0:T(8,128)(2,1)} fusion(f32[32,8,128]{2,1,0:T(8,128)S(1)} %convolution_bitcast_fusion, bf16[32,8,64]{2,1,0:T(8,128)(2,1)S(1)} %fusion.3, bf16[32,64,128]{2,1,0:T(8,128)(2,1)S(1)} %copy-done.1), kind=kOutput, calls=%fused_computation.6 | convolution fusion | flops 4259840 | bytes 753664 | tf_op jit(solution)/shard_map/lrk,lkp->lrp/dot_general | solution.py:124
  (48 shorter events, 1.8 us)
Async XLA Ops:
  0.0 43.7 %copy-start = (bf16[32,64,384]{2,1,0:T(8,128)(2,1)S(1)}, bf16[32,64,384]{2,1,0:T(8,128)(2,1)}, u32[]{:S(2)}) copy-start(bf16[32,64,384]{2,1,0:T(8,128)(2,1)} %param.14) | copy-start | bytes 4718596
  2.6 39.4 %collective-permute-start.1 = (bf16[32,1536]{1,0:T(8,128)(2,1)S(1)}, bf16[32,1536]{1,0:T(8,128)(2,1)S(1)}, u32[]{:S(2)}, u32[]{:S(2)}) collective-permute-start(bf16[32,1536]{1,0:T(8,128)(2,1)S(1)} %constant_dynamic-update-slice_fusion), channel_id=1, source_target_pairs={{1,2},{3,4},{5,6},{7,8},{9,10},{11,12},{13,14},{15,16},{17,18},{19... | collective-permute-start | bytes 294920 | tf_op jit(solution)/shard_map/ppermute | solution.py:62
  9.6 32.0 %collective-permute-start = (bf16[33,1536]{1,0:T(8,128)(2,1)S(1)}, bf16[33,1536]{1,0:T(8,128)(2,1)S(1)}, u32[]{:S(2)}, u32[]{:S(2)}) collective-permute-start(bf16[33,1536]{1,0:T(8,128)(2,1)S(1)} %fusion.4), channel_id=1, source_target_pairs={{0,1},{1,0},{2,3},{3,2},{4,5},{5,4},{6,7},{7,6},{8,9},{9,8},{10,11... | collective-permute-start | bytes 304136 | tf_op jit(solution)/shard_map/ppermute | solution.py:63
  36.1 14.6 %all-to-all-start = ((bf16[16,32,512]{2,1,0:T(8,128)(2,1)}), bf16[16,32,512]{2,1,0:T(8,128)(2,1)S(1)}, u32[]{:S(2)}, u32[]{:S(2)}) async-start(bf16[16,32,512]{2,1,0:T(8,128)(2,1)} %broadcast_in_dim.30), calls=%async_computation | async-start | bytes 1048576 | tf_op jit(solution)/shard_map/all_to_all | solution.py:49
  45.1 14.0 %copy-start.2 = (bf16[4,64,512]{2,1,0:T(8,128)(2,1)S(1)}, bf16[4,64,512]{2,1,0:T(8,128)(2,1)}, u32[]{:S(2)}) copy-start(bf16[4,64,512]{2,1,0:T(8,128)(2,1)} %param.15) | copy-start | bytes 786436
  45.1 14.5 %copy-start.1 = (bf16[32,64,128]{2,1,0:T(8,128)(2,1)S(1)}, bf16[32,64,128]{2,1,0:T(8,128)(2,1)}, u32[]{:S(2)}) copy-start(bf16[32,64,128]{2,1,0:T(8,128)(2,1)} %param.10) | copy-start | bytes 1572868
  46.2 12.9 %copy-start.4 = (bf16[4,64,512]{2,1,0:T(8,128)(2,1)S(1)}, bf16[4,64,512]{2,1,0:T(8,128)(2,1)}, u32[]{:S(2)}) copy-start(bf16[4,64,512]{2,1,0:T(8,128)(2,1)} %param.17) | copy-start | bytes 786436
  46.2 13.3 %copy-start.3 = (f32[32,8,64]{2,1,0:T(8,128)S(1)}, f32[32,8,64]{2,1,0:T(8,128)}, u32[]{:S(2)}) copy-start(f32[32,8,64]{2,1,0:T(8,128)} %fusion.44) | copy-start | bytes 196612
  51.4 7.3 %collective-permute-start.2 = (bf16[4,8,512]{2,1,0:T(8,128)(2,1)S(1)}, bf16[4,8,512]{2,1,0:T(8,128)(2,1)S(1)}, u32[]{:S(2)}, u32[]{:S(2)}) collective-permute-start(bf16[4,8,512]{2,1,0:T(8,128)(2,1)S(1)} %bitcast.55), channel_id=1, source_target_pairs={{0,1},{1,0},{2,3},{3,2},{4,5},{5,4},{6,7},{7,6},{8,9},{9,8},{10,11... | collective-permute-start | bytes 98312 | tf_op jit(solution)/shard_map/ppermute | solution.py:107

commit v4 on v2

--- a/solution.py
+++ b/solution.py
@@ -78,8 +78,12 @@
     near_rows = jnp.take(density_padded, halo_row(near_list), axis=0, mode="clip").reshape(
         leaf_count, near_list.shape[1], rhs_count, leaf_width
     )
-    near_part = jnp.einsum(
-        "ljpq,ljrq->lrp", near_blocks, near_rows, preferred_element_type=jnp.float32
+    half = leaf_count // 2
+    near_early = jnp.einsum(
+        "ljpq,ljrq->lrp", near_blocks[:half], near_rows[:half], preferred_element_type=jnp.float32
+    )
+    near_late = jnp.einsum(
+        "ljpq,ljrq->lrp", near_blocks[half:], near_rows[half:], preferred_element_type=jnp.float32
     )
     far_skels = jnp.take(skeleton_padded, halo_row(far_leaf), axis=0, mode="clip").reshape(
         leaf_count, far_count, rhs_count, rank_width
@@ -87,7 +91,9 @@
     leaf_far = jnp.einsum(
         "lkq,lrq->lrk", leaf_coupling, side_by_side(far_skels), preferred_element_type=jnp.float32
     )
-    everything, near_part, leaf_far = lax.optimization_barrier((everything, near_part, leaf_far))
+    everything, near_early, leaf_far = lax.optimization_barrier((everything, near_early, leaf_far))
+    near_late = lax.optimization_barrier(near_late)
+    near_part = jnp.concatenate([near_early, near_late], axis=0)
 
     def placed(boxes):
         owner, slot = boxes // box_count, boxes % box_count

time: 43.8 us -> 48.5 us (1.11)
  matrix products: 9.68 us -> 12.3 us
  waiting for transfers between devices: 0.53 us -> 2.04 us
  local copies, waits for them, and re-layouts: 7.83 us -> 8.46 us
    dot_general x1 -> x2, matrix products: 4.55 us -> 6.92 us  [the longest x1 3.49 us: body(): jnp.einsum('ljpq,ljrq->lrp', near_blocks[:half], near_rows[:half], prefer...]
    all_to_all x2, waiting for transfers between devices: 0.3 us -> 2.03 us  [body(): moved = lax.all_to_all(spread, axes, 0, 0, tiled=False)]
    dot_general x1, matrix products: 0.88 us -> 1.75 us  [body(): jnp.einsum('lrk,lkp->lrp', local_field, basis, preferred_element_type=jnp...]
    dot_general x1, matrix products: 1.3 us -> 0.64 us  [body(): jnp.einsum('lkq,lrq->lrk', leaf_coupling, side_by_side(far_skels), prefer...]
    gather x1, local copies, waits for them, and re-layouts: 0.63 us -> 1.24 us  [body(): jnp.take(everything, asked, axis=0, mode='clip')]
  transfers between devices with their start and end apart: 5 -> 5, of which waited for: 2 -> 1; matrix products, arithmetic and copies ran while one was open for 33% -> 33% of each run, Pallas kernels for 0% -> 0%
where the time goes in v4:
time: 48.5 us; the launch traced here: 48 us
  starting transfers between devices  22.4 us (46%)
  matrix products  12.3 us (25%)
  local copies, waits for them, and re-layouts  8.46 us (17%)
  other arithmetic  2.47 us (5%)
  waiting for transfers between devices  2.04 us (4%)
    all_to_all x2, starting transfers between devices, body(): moved = lax.all_to_all(spread, axes, 0, 0, tiled=False)  13.7 us
    ppermute x1, starting transfers between devices, body(): cross = lax.ppermute(own, ALL, cross_pairs)  5.66 us
    dot_general x1, matrix products, body(): jnp.einsum('ljpq,ljrq->lrp', near_blocks[:half], near_rows[:half], prefer...  3.49 us
    dot_general x1, matrix products, body(): jnp.einsum('ljpq,ljrq->lrp', near_blocks[half:], near_rows[half:], prefer...  3.43 us
    ppermute x1, starting transfers between devices, body(): lax.ppermute(jnp.take(everything, asked, axis=0, mode='clip'), PAIR, [(0,...  2.95 us
    all_to_all x2, waiting for transfers between devices, body(): moved = lax.all_to_all(spread, axes, 0, 0, tiled=False)  2.03 us
    dot_general x1, matrix products, body(): jnp.einsum('lrk,lkp->lrp', local_field, basis, preferred_element_type=jnp...  1.75 us
    broadcast_in_dim x4, local copies, waits for them, and re-layouts, body(): spread = jnp.broadcast_to(everything[None], (n,) + everything.shape)  1.59 us
  transfers between devices with their start and end apart: 5, of which 1 were waited for; matrix products, arithmetic and copies ran while one was open for 33% of the time, Pallas kernels for 0%

profile of v4, /device:TPU:1, one launch (start us, length us, event | category | flops | bytes accessed | tf_op | source)
XLA Modules:
  0.0 48.0 jit_solution(4660209596459917595)
XLA Ops:
  0.0 1.6 %convolution_convert_fusion = bf16[32,8,64]{2,1,0:T(8,128)(2,1)S(1)} fusion(bf16[32,8,128]{2,1,0:T(8,128)(2,1)} %param.9, bf16[32,64,128]{2,1,0:T(8,128)(2,1)} %param.10), kind=kOutput, calls=%fused_computation.10 | convolution fusion | flops 4210688 | bytes 622592 | tf_op jit(solution)/shard_map/lrp,lkp->lrk/dot_general | solution.py:34
  1.7 1.1 %convolution_convert_fusion.2 = bf16[4,8,64]{2,1,0:T(8,128)(2,1)S(1)} fusion(bf16[4,8,512]{2,1,0:T(8,128)(2,1)S(1)} %reshape.69, bf16[4,64,512]{2,1,0:T(8,128)(2,1)} %param.15), kind=kOutput, calls=%fused_computation.14 | convolution fusion | flops 2099200 | bytes 299008 | tf_op jit(solution)/shard_map/ckq,crq->crk/dot_general | solution.py:38
  2.9 0.6 %broadcast_in_dim.39 = bf16[8,4,512]{2,1,0:T(4,128)(2,1)} broadcast(bf16[4,512]{1,0:T(4,128)(2,1)S(1)} %broadcast_in_dim.38), dimensions={1,2} | broadcast | bytes 36864 | tf_op jit(solution)/shard_map/broadcast_in_dim | solution.py:45
  3.6 9.0 %all-to-all-start = ((bf16[8,4,512]{2,1,0:T(4,128)(2,1)}), bf16[8,4,512]{2,1,0:T(4,128)(2,1)S(1)}, u32[]{:S(2)}, u32[]{:S(2)}) async-start(bf16[8,4,512]{2,1,0:T(4,128)(2,1)} %broadcast_in_dim.39), calls=%async_computation | async-start | bytes 65536 | tf_op jit(solution)/shard_map/all_to_all | solution.py:46
  12.7 0.8 %bitcast_dynamic-update-slice_fusion = bf16[32,1536]{1,0:T(8,128)(2,1)S(1)} fusion(bf16[4,8,8,128]{3,2,1,0:T(8,128)(2,1)} %bitcast.61), kind=kLoop, calls=%fused_computation.26 | loop fusion | bytes 131072
  13.6 5.7 %collective-permute-start.1 = (bf16[32,1536]{1,0:T(8,128)(2,1)S(1)}, bf16[32,1536]{1,0:T(8,128)(2,1)S(1)}, u32[]{:S(2)}, u32[]{:S(2)}) collective-permute-start(bf16[32,1536]{1,0:T(8,128)(2,1)S(1)} %constant_dynamic-update-slice_fusion), channel_id=1, source_target_pairs={{1,2},{3,4},{5,6},{7,8},{9,10},{11,12},{13,14},{15,16},{17,18},{19... | collective-permute-start | bytes 294920 | tf_op jit(solution)/shard_map/ppermute | solution.py:61
  19.2 0.7 %fusion.37 = (s32[4,8]{1,0:T(4,128)S(1)}, bf16[1,4,8]{2,1,0:T(4,128)(2,1)S(1)}, bf16[1,4,8]{2,1,0:T(4,128)(2,1)S(1)}) fusion(s32[4,8]{1,0:T(4,128)} %param.16), kind=kLoop, calls=%fused_computation.116 | loop fusion | flops 4032 | bytes 384 | tf_op jit(solution)/shard_map/add | solution.py:108
  20.2 0.7 %fusion.19 = pred[4,8]{1,0:T(4,128)(4,1)S(1)} fusion(s32[]{:T(128)S(6)} %axis_index.60, s32[4,8]{1,0:T(4,128)} %param.16), kind=kLoop, calls=%fused_computation.98 | loop fusion | flops 864 | bytes 164 | tf_op jit(solution)/shard_map/ne | solution.py:108
  21.0 0.7 %fusion.15 = (s32[32,6]{0,1:T(8,128)S(1)}, s32[32,6]{0,1:T(8,128)S(1)}) fusion(s32[32,6]{0,1:T(8,128)} %param.11, s32[]{:T(128)S(6)} %mul.49, pred[]{:T(512)S(6)} %eq.16, s32[32,6]{0,1:T(8,128)} %param.13), kind=kLoop, calls=%fused_computation.30 | loop fusion | flops 3840 | bytes 3077 | tf_op jit(solution)/shard_map/jit(_where)/select_n | solution.py:76
  22.2 0.8 %broadcast_in_dim.41 = bf16[16,32,512]{2,1,0:T(8,128)(2,1)} broadcast(bf16[32,512]{1,0:T(8,128)(2,1)S(1)} %broadcast_in_dim.40), dimensions={1,2} | broadcast | bytes 557056 | tf_op jit(solution)/shard_map/broadcast_in_dim | solution.py:45
  23.0 4.7 %all-to-all-start.1 = ((bf16[16,32,512]{2,1,0:T(8,128)(2,1)}), bf16[16,32,512]{2,1,0:T(8,128)(2,1)S(1)}, u32[]{:S(2)}, u32[]{:S(2)}) async-start(bf16[16,32,512]{2,1,0:T(8,128)(2,1)} %broadcast_in_dim.41), calls=%async_computation.1 | async-start | bytes 1048576 | tf_op jit(solution)/shard_map/all_to_all | solution.py:46
  28.1 1.0 %gather_fusion = bf16[192,1024]{1,0:T(8,128)(2,1)S(1)} fusion(bf16[96,1024]{1,0:T(8,128)(2,1)S(1)} %slice.65, s32[1024]{0:T(1024)S(1)} %pad_clamp_fusion.3), kind=kCustom, calls=%fused_computation | custom fusion | bytes 787200 | tf_op jit(solution)/shard_map/jit(_take)/gather | solution.py:78
  29.3 1.0 %gather_fusion.1 = bf16[192,512]{1,0:T(8,128)(2,1)S(1)} fusion(bf16[96,512]{1,0:T(8,128)(2,1)S(1)} %pad_maximum_fusion.1, s32[1024]{0:T(1024)S(1)} %pad_clamp_fusion.2), kind=kCustom, calls=%fused_computation.1 | custom fusion | bytes 393984 | tf_op jit(solution)/shard_map/jit(_take)/gather | solution.py:88
  30.3 0.2 reshape.73
  30.6 0.3 reshape.74
  31.0 0.6 %fusion.54 = f32[32,8,64]{2,1,0:T(8,128)S(1)} fusion(bf16[32,8,384]{2,1,0:T(8,128)(2,1)S(1)} %reshape.74, bf16[32,64,384]{2,1,0:T(8,128)(2,1)S(1)} %copy-done), kind=kOutput, calls=%fused_computation.148 | convolution fusion | flops 12582912 | bytes 1835008 | tf_op jit(solution)/shard_map/lkq,lrq->lrk/dot_general | solution.py:91
  31.6 3.5 %fusion.5 = f32[16,8,128]{2,1,0:T(8,128)} fusion(bf16[16,6,8,128]{3,2,1,0:T(8,128)(2,1)S(1)} %bitcast.59, bf16[32,6,128,128]{3,2,1,0:T(8,128)(2,1)} %param.12), kind=kOutput, calls=%fused_computation.11 | convolution fusion | flops 25165824 | bytes 3407872 | tf_op jit(solution)/shard_map/ljpq,ljrq->lrp/dot_general | solution.py:82
  35.1 2.0 %all-to-all-done.1 = bf16[16,32,512]{2,1,0:T(8,128)(2,1)S(1)} async-done(((bf16[16,32,512]{2,1,0:T(8,128)(2,1)}), bf16[16,32,512]{2,1,0:T(8,128)(2,1)S(1)}, u32[]{:S(2)}, u32[]{:S(2)}) %all-to-all-start.1) | async-done | bytes 524320 | tf_op jit(solution)/shard_map/all_to_all | solution.py:46
  37.1 1.2 %gather_fusion.2 = bf16[32,512]{1,0:T(8,128)(2,1)} fusion(bf16[512,512]{1,0:T(8,128)(2,1)S(1)} %bitcast.56, s32[1024]{0:T(1024)S(1)} %pad_clamp_fusion.1), kind=kCustom, calls=%fused_computation.2 | custom fusion | bytes 65664 | tf_op jit(solution)/shard_map/jit(_take)/gather | solution.py:112
  38.4 3.0 %collective-permute-start.2 = (bf16[4,8,512]{2,1,0:T(8,128)(2,1)}, bf16[4,8,512]{2,1,0:T(8,128)(2,1)S(1)}, u32[]{:S(2)}, u32[]{:S(2)}) collective-permute-start(bf16[4,8,512]{2,1,0:T(8,128)(2,1)} %bitcast.8), channel_id=1, source_target_pairs={{0,1},{1,0},{2,3},{3,2},{4,5},{5,4},{6,7},{7,6},{8,9},{9,8},{10,11... | collective-permute-start | bytes 98312 | tf_op jit(solution)/shard_map/ppermute | solution.py:112
  41.3 3.4 %fusion.8 = f32[16,8,128]{2,1,0:T(8,128)} fusion(bf16[16,6,8,128]{3,2,1,0:T(8,128)(2,1)S(1)} %bitcast.58, bf16[32,6,128,128]{3,2,1,0:T(8,128)(2,1)} %param.12), kind=kOutput, calls=%fused_computation.12 | convolution fusion | flops 25165824 | bytes 3407872 | tf_op jit(solution)/shard_map/ljpq,ljrq->lrp/dot_general | solution.py:85
  44.8 0.6 %gather_fusion.3 = bf16[32,512]{1,0:T(8,128)(2,1)S(1)} fusion(bf16[512,512]{1,0:T(8,128)(2,1)S(1)} %bitcast.57, s32[1024]{0:T(1024)S(1)} %pad_clamp_fusion), kind=kCustom, calls=%fused_computation.3 | custom fusion | bytes 65664 | tf_op jit(solution)/shard_map/jit(_take)/gather | solution.py:114
  45.8 0.3 fusion.11
  46.2 1.8 %fusion.4 = bf16[32,8,128]{2,1,0:T(8,128)(2,1)} fusion(bf16[32,8,64]{2,1,0:T(8,128)(2,1)S(1)} %fusion.13, bf16[32,64,128]{2,1,0:T(8,128)(2,1)S(1)} %copy-done.1, f32[16,8,128]{2,1,0:T(8,128)} %fusion.8, f32[16,8,128]{2,1,0:T(8,128)} %fusion.5), kind=kOutput, calls=%fused_computation.9 | convolution fusion | flops 4292608 | bytes 753664 | tf_op jit(solution)/shard_map/lrk,lkp->lrp/dot_general | solution.py:129
  (51 shorter events, 2.1 us)
Async XLA Ops:
  0.0 31.0 %copy-start = (bf16[32,64,384]{2,1,0:T(8,128)(2,1)S(1)}, bf16[32,64,384]{2,1,0:T(8,128)(2,1)}, u32[]{:S(2)}) copy-start(bf16[32,64,384]{2,1,0:T(8,128)(2,1)} %param.14) | copy-start | bytes 4718596
  3.6 18.6 %all-to-all-start = ((bf16[8,4,512]{2,1,0:T(4,128)(2,1)}), bf16[8,4,512]{2,1,0:T(4,128)(2,1)S(1)}, u32[]{:S(2)}, u32[]{:S(2)}) async-start(bf16[8,4,512]{2,1,0:T(4,128)(2,1)} %broadcast_in_dim.39), calls=%async_computation | async-start | bytes 65536 | tf_op jit(solution)/shard_map/all_to_all | solution.py:46
  13.6 14.5 %collective-permute-start.1 = (bf16[32,1536]{1,0:T(8,128)(2,1)S(1)}, bf16[32,1536]{1,0:T(8,128)(2,1)S(1)}, u32[]{:S(2)}, u32[]{:S(2)}) collective-permute-start(bf16[32,1536]{1,0:T(8,128)(2,1)S(1)} %constant_dynamic-update-slice_fusion), channel_id=1, source_target_pairs={{1,2},{3,4},{5,6},{7,8},{9,10},{11,12},{13,14},{15,16},{17,18},{19... | collective-permute-start | bytes 294920 | tf_op jit(solution)/shard_map/ppermute | solution.py:61
  20.1 7.6 %collective-permute-start = (bf16[33,1536]{1,0:T(8,128)(2,1)S(1)}, bf16[33,1536]{1,0:T(8,128)(2,1)S(1)}, u32[]{:S(2)}, u32[]{:S(2)}) collective-permute-start(bf16[33,1536]{1,0:T(8,128)(2,1)S(1)} %fusion.14), channel_id=1, source_target_pairs={{0,1},{1,0},{2,3},{3,2},{4,5},{5,4},{6,7},{7,6},{8,9},{9,8},{10,11... | collective-permute-start | bytes 304136 | tf_op jit(solution)/shard_map/ppermute | solution.py:62
  23.0 14.1 %all-to-all-start.1 = ((bf16[16,32,512]{2,1,0:T(8,128)(2,1)}), bf16[16,32,512]{2,1,0:T(8,128)(2,1)S(1)}, u32[]{:S(2)}, u32[]{:S(2)}) async-start(bf16[16,32,512]{2,1,0:T(8,128)(2,1)} %broadcast_in_dim.41), calls=%async_computation.1 | async-start | bytes 1048576 | tf_op jit(solution)/shard_map/all_to_all | solution.py:46
  31.6 14.1 %copy-start.2 = (bf16[4,64,512]{2,1,0:T(8,128)(2,1)S(1)}, bf16[4,64,512]{2,1,0:T(8,128)(2,1)}, u32[]{:S(2)}) copy-start(bf16[4,64,512]{2,1,0:T(8,128)(2,1)} %param.15) | copy-start | bytes 786436
  35.1 10.6 %copy-start.3 = (bf16[4,64,512]{2,1,0:T(8,128)(2,1)S(1)}, bf16[4,64,512]{2,1,0:T(8,128)(2,1)}, u32[]{:S(2)}) copy-start(bf16[4,64,512]{2,1,0:T(8,128)(2,1)} %param.17) | copy-start | bytes 786436
  35.1 11.1 %copy-start.1 = (bf16[32,64,128]{2,1,0:T(8,128)(2,1)S(1)}, bf16[32,64,128]{2,1,0:T(8,128)(2,1)}, u32[]{:S(2)}) copy-start(bf16[32,64,128]{2,1,0:T(8,128)(2,1)} %param.10) | copy-start | bytes 1572868
  38.4 7.0 %collective-permute-start.2 = (bf16[4,8,512]{2,1,0:T(8,128)(2,1)}, bf16[4,8,512]{2,1,0:T(8,128)(2,1)S(1)}, u32[]{:S(2)}, u32[]{:S(2)}) collective-permute-start(bf16[4,8,512]{2,1,0:T(8,128)(2,1)} %bitcast.8), channel_id=1, source_target_pairs={{0,1},{1,0},{2,3},{3,2},{4,5},{5,4},{6,7},{7,6},{8,9},{9,8},{10,11... | collective-permute-start | bytes 98312 | tf_op jit(solution)/shard_map/ppermute | solution.py:112

commit v5 on v1

--- a/solution.py
+++ b/solution.py
@@ -75,13 +75,15 @@
         high = jnp.where(even, t - leaf_count, t + leaf_count)
         return jnp.where(t < 0, low, jnp.where(t < leaf_count, t + leaf_count, high))
 
-    near_rows = jnp.take(density_padded, halo_row(near_list), axis=0).reshape(
+    near_index, far_index = halo_row(near_list), halo_row(far_leaf)
+
+    near_rows = jnp.take(density_padded, near_index, axis=0).reshape(
         leaf_count, near_list.shape[1], rhs_count, leaf_width
     )
     near_part = jnp.einsum(
         "ljpq,ljrq->lrp", near_blocks, near_rows, preferred_element_type=jnp.float32
     )
-    far_skels = jnp.take(skeleton_padded, halo_row(far_leaf), axis=0).reshape(
+    far_skels = jnp.take(skeleton_padded, far_index, axis=0).reshape(
         leaf_count, far_count, rhs_count, rank_width
     )
     leaf_far = jnp.einsum(

time: 44 us -> 44 us (level)
  no operation moved by 1% of the time
where the time goes in v5:
time: 44 us; the launch traced here: 43.6 us
  starting transfers between devices  22.2 us (50%)
  matrix products  9.73 us (22%)
  local copies, waits for them, and re-layouts  7.92 us (18%)
  other arithmetic  2.67 us (6%)
  waiting for transfers between devices  0.78 us (2%)
    all_to_all x2, starting transfers between devices, body(): moved = lax.all_to_all(spread, axes, 0, 0, tiled=False)  13.7 us
    ppermute x1, starting transfers between devices, body(): cross = lax.ppermute(own, ALL, cross_pairs)  5.66 us
    dot_general x1, matrix products, body(): jnp.einsum('ljpq,ljrq->lrp', near_blocks, near_rows, preferred_element_ty...  4.6 us
    ppermute x1, starting transfers between devices, body(): lax.ppermute(jnp.take(everything, asked, axis=0), PAIR, [(0, 1), (1, 0)])  2.71 us
    broadcast_in_dim x4, local copies, waits for them, and re-layouts, body(): spread = jnp.broadcast_to(everything[None], (n,) + everything.shape)  1.6 us
    dot_general x1, matrix products, body(): jnp.einsum('lrp,lkp->lrk', density, basis, preferred_element_type=jnp.flo...  1.56 us
    dot_general x1, matrix products, body(): jnp.einsum('lkq,lrq->lrk', leaf_coupling, side_by_side(far_skels), prefer...  1.3 us
    gather x2, local copies, waits for them, and re-layouts, body(): jnp.take(skeleton_padded, far_index, axis=0)  1.22 us
  transfers between devices with their start and end apart: 5, of which 2 were waited for; matrix products, arithmetic and copies ran while one was open for 33% of the time, Pallas kernels for 0%

profile of v5, /device:TPU:1, one launch (start us, length us, event | category | flops | bytes accessed | tf_op | source)
XLA Modules:
  0.0 43.6 jit_solution(2355332595567026922)
XLA Ops:
  0.0 1.6 %convolution_convert_fusion = bf16[32,8,64]{2,1,0:T(8,128)(2,1)S(1)} fusion(bf16[32,8,128]{2,1,0:T(8,128)(2,1)} %param.11, bf16[32,64,128]{2,1,0:T(8,128)(2,1)} %param.12), kind=kOutput, calls=%fused_computation.7 | convolution fusion | flops 4210688 | bytes 622592 | tf_op jit(solution)/shard_map/lrp,lkp->lrk/dot_general | solution.py:34
  1.7 1.1 %convolution_convert_fusion.2 = bf16[4,8,64]{2,1,0:T(8,128)(2,1)S(1)} fusion(bf16[4,8,512]{2,1,0:T(8,128)(2,1)S(1)} %reshape.82, bf16[4,64,512]{2,1,0:T(8,128)(2,1)} %param.17), kind=kOutput, calls=%fused_computation.9 | convolution fusion | flops 2099200 | bytes 299008 | tf_op jit(solution)/shard_map/ckq,crq->crk/dot_general | solution.py:38
  2.9 0.6 %broadcast_in_dim.57 = bf16[8,4,512]{2,1,0:T(4,128)(2,1)} broadcast(bf16[4,512]{1,0:T(4,128)(2,1)S(1)} %broadcast_in_dim.56), dimensions={1,2} | broadcast | bytes 36864 | tf_op jit(solution)/shard_map/broadcast_in_dim | solution.py:45
  3.6 9.0 %all-to-all-start = ((bf16[8,4,512]{2,1,0:T(4,128)(2,1)}), bf16[8,4,512]{2,1,0:T(4,128)(2,1)S(1)}, u32[]{:S(2)}, u32[]{:S(2)}) async-start(bf16[8,4,512]{2,1,0:T(4,128)(2,1)} %broadcast_in_dim.57), calls=%async_computation | async-start | bytes 65536 | tf_op jit(solution)/shard_map/all_to_all | solution.py:46
  12.7 0.8 %bitcast_dynamic-update-slice_fusion = bf16[32,1536]{1,0:T(8,128)(2,1)S(1)} fusion(bf16[4,8,8,128]{3,2,1,0:T(8,128)(2,1)} %bitcast.53), kind=kLoop, calls=%fused_computation.23 | loop fusion | bytes 131072
  13.6 5.7 %collective-permute-start.1 = (bf16[32,1536]{1,0:T(8,128)(2,1)S(1)}, bf16[32,1536]{1,0:T(8,128)(2,1)S(1)}, u32[]{:S(2)}, u32[]{:S(2)}) collective-permute-start(bf16[32,1536]{1,0:T(8,128)(2,1)S(1)} %constant_dynamic-update-slice_fusion), channel_id=1, source_target_pairs={{1,2},{3,4},{5,6},{7,8},{9,10},{11,12},{13,14},{15,16},{17,18},{19... | collective-permute-start | bytes 294920 | tf_op jit(solution)/shard_map/ppermute | solution.py:61
  19.2 0.7 %fusion.48 = (bf16[1,4,8]{2,1,0:T(4,128)(2,1)S(1)}, bf16[1,4,8]{2,1,0:T(4,128)(2,1)S(1)}) fusion(s32[4,8]{1,0:T(4,128)} %param.18), kind=kLoop, calls=%fused_computation.152 | loop fusion | flops 672 | bytes 256 | tf_op jit(solution)/shard_map/stack | solution.py:57
  20.1 0.7 %compare_and_fusion.2 = (pred[4,8]{1,0:T(4,128)(4,1)S(1)}, s32[4,8]{1,0:T(4,128)S(1)}, pred[4,8]{1,0:T(4,128)(4,1)S(1)}) fusion(s32[4,8]{1,0:T(4,128)} %param.18, s32[]{:T(128)S(6)} %axis_index.60), kind=kLoop, calls=%fused_computation.143 | loop fusion | flops 3872 | bytes 324 | tf_op jit(solution)/shard_map/jit(_take)/and | solution.py:110
  21.0 0.7 %compare_and_fusion = (pred[32,6]{0,1:T(8,128)(4,1)S(1)}, s32[32,6]{0,1:T(8,128)S(1)}, pred[32,6]{0,1:T(8,128)(4,1)S(1)}, s32[32,6]{0,1:T(8,128)S(1)}) fusion(pred[]{:T(512)S(6)} %eq.16, s32[32,6]{0,1:T(8,128)} %param.15, s32[]{:T(128)S(6)} %mul.49, s32[32,6]{0,1:T(8,128)} %param.13), kind=kLoop, calls=%fused_computation.40 | loop fusion | flops 6144 | bytes 3461 | tf_op jit(solution)/shard_map/jit(_take)/and | solution.py:86
  22.4 0.8 %broadcast_in_dim.59 = bf16[16,32,512]{2,1,0:T(8,128)(2,1)} broadcast(bf16[32,512]{1,0:T(8,128)(2,1)S(1)} %broadcast_in_dim.58), dimensions={1,2} | broadcast | bytes 557056 | tf_op jit(solution)/shard_map/broadcast_in_dim | solution.py:45
  23.2 4.7 %all-to-all-start.1 = ((bf16[16,32,512]{2,1,0:T(8,128)(2,1)}), bf16[16,32,512]{2,1,0:T(8,128)(2,1)S(1)}, u32[]{:S(2)}, u32[]{:S(2)}) async-start(bf16[16,32,512]{2,1,0:T(8,128)(2,1)} %broadcast_in_dim.59), calls=%async_computation.1 | async-start | bytes 1048576 | tf_op jit(solution)/shard_map/all_to_all | solution.py:46
  28.3 1.0 %gather_fusion.1 = bf16[192,512]{1,0:T(8,128)(2,1)S(1)} fusion(bf16[96,512]{1,0:T(8,128)(2,1)S(1)} %pad_maximum_fusion.1, s32[1024]{0:T(1024)S(1)} %pad_clamp_fusion.2), kind=kCustom, calls=%fused_computation.3 | custom fusion | bytes 393984 | tf_op jit(solution)/shard_map/jit(_take)/gather | solution.py:86
  29.3 0.2 gather.18
  29.7 0.3 reshape.86
  30.0 1.3 %fusion.50 = f32[32,8,64]{2,1,0:T(8,128)} fusion(bf16[32,8,384]{2,1,0:T(8,128)(2,1)S(1)} %reshape.86, bf16[32,64,384]{2,1,0:T(8,128)(2,1)S(1)} %copy-done), kind=kOutput, calls=%fused_computation.156 | convolution fusion | flops 12582912 | bytes 1835008 | tf_op jit(solution)/shard_map/lkq,lrq->lrk/dot_general | solution.py:89
  31.4 1.0 %gather_fusion = bf16[192,1024]{1,0:T(8,128)(2,1)S(1)} fusion(bf16[96,1024]{1,0:T(8,128)(2,1)S(1)} %slice.39, s32[1024]{0:T(1024)S(1)} %pad_clamp_fusion.3), kind=kCustom, calls=%fused_computation.2 | custom fusion | bytes 787200 | tf_op jit(solution)/shard_map/jit(_take)/gather | solution.py:80
  32.5 4.6 %convolution_bitcast_fusion = f32[32,8,128]{2,1,0:T(8,128)S(1)} fusion(bf16[32,6,128,128]{3,2,1,0:T(8,128)(2,1)} %param.14, bf16[32,6,8,128]{3,2,1,0:T(8,128)(2,1)S(1)} %bitcast.51, pred[32,6]{1,0:T(8,128)(4,1)S(1)} %copy.23), kind=kOutput, calls=%fused_computation.5 | convolution fusion | flops 50528256 | bytes 6815936 | tf_op jit(solution)/shard_map/ljpq,ljrq->lrp/dot_general | solution.py:83
  37.1 0.5 %all-to-all-done.1 = bf16[16,32,512]{2,1,0:T(8,128)(2,1)S(1)} async-done(((bf16[16,32,512]{2,1,0:T(8,128)(2,1)}), bf16[16,32,512]{2,1,0:T(8,128)(2,1)S(1)}, u32[]{:S(2)}, u32[]{:S(2)}) %all-to-all-start.1) | async-done | bytes 524320 | tf_op jit(solution)/shard_map/all_to_all | solution.py:46
  37.6 0.6 %gather_fusion.2 = bf16[32,512]{1,0:T(8,128)(2,1)S(1)} fusion(bf16[512,512]{1,0:T(8,128)(2,1)S(1)} %bitcast.49, s32[1024]{0:T(1024)S(1)} %pad_clamp_fusion.1), kind=kCustom, calls=%fused_computation.clone | custom fusion | bytes 65664 | tf_op jit(solution)/shard_map/jit(_take)/gather | solution.py:108
  38.3 2.7 %collective-permute-start.2 = (bf16[4,8,512]{2,1,0:T(8,128)(2,1)S(1)}, bf16[4,8,512]{2,1,0:T(8,128)(2,1)S(1)}, u32[]{:S(2)}, u32[]{:S(2)}) collective-permute-start(bf16[4,8,512]{2,1,0:T(8,128)(2,1)S(1)} %bitcast_select_fusion.1), channel_id=1, source_target_pairs={{0,1},{1,0},{2,3},{3,2},{4,5},{5,4},{6,7},{7,6},{8,9},{9,8},{10,11... | collective-permute-start | bytes 98312 | tf_op jit(solution)/shard_map/ppermute | solution.py:108
  41.1 0.6 %gather_fusion.3 = bf16[32,512]{1,0:T(8,128)(2,1)S(1)} fusion(bf16[512,512]{1,0:T(8,128)(2,1)S(1)} %bitcast.50, s32[1024]{0:T(1024)S(1)} %pad_clamp_fusion), kind=kCustom, calls=%fused_computation.1.clone | custom fusion | bytes 65664 | tf_op jit(solution)/shard_map/jit(_take)/gather | solution.py:110
  41.7 0.2 collective-permute-done.2
  42.3 0.3 fusion.1
  42.7 0.9 %fusion = bf16[32,8,128]{2,1,0:T(8,128)(2,1)} fusion(f32[32,8,128]{2,1,0:T(8,128)S(1)} %convolution_bitcast_fusion, bf16[32,8,64]{2,1,0:T(8,128)(2,1)S(1)} %fusion.7, bf16[32,64,128]{2,1,0:T(8,128)(2,1)S(1)} %copy-done.1), kind=kOutput, calls=%fused_computation.6 | convolution fusion | flops 4259840 | bytes 753664 | tf_op jit(solution)/shard_map/lrk,lkp->lrp/dot_general | solution.py:125
  (53 shorter events, 2.4 us)
Async XLA Ops:
  0.0 30.0 %copy-start = (bf16[32,64,384]{2,1,0:T(8,128)(2,1)S(1)}, bf16[32,64,384]{2,1,0:T(8,128)(2,1)}, u32[]{:S(2)}) copy-start(bf16[32,64,384]{2,1,0:T(8,128)(2,1)} %param.16) | copy-start | bytes 4718596
  3.6 18.8 %all-to-all-start = ((bf16[8,4,512]{2,1,0:T(4,128)(2,1)}), bf16[8,4,512]{2,1,0:T(4,128)(2,1)S(1)}, u32[]{:S(2)}, u32[]{:S(2)}) async-start(bf16[8,4,512]{2,1,0:T(4,128)(2,1)} %broadcast_in_dim.57), calls=%async_computation | async-start | bytes 65536 | tf_op jit(solution)/shard_map/all_to_all | solution.py:46
  13.6 14.7 %collective-permute-start.1 = (bf16[32,1536]{1,0:T(8,128)(2,1)S(1)}, bf16[32,1536]{1,0:T(8,128)(2,1)S(1)}, u32[]{:S(2)}, u32[]{:S(2)}) collective-permute-start(bf16[32,1536]{1,0:T(8,128)(2,1)S(1)} %constant_dynamic-update-slice_fusion), channel_id=1, source_target_pairs={{1,2},{3,4},{5,6},{7,8},{9,10},{11,12},{13,14},{15,16},{17,18},{19... | collective-permute-start | bytes 294920 | tf_op jit(solution)/shard_map/ppermute | solution.py:61
  20.0 7.9 %collective-permute-start = (bf16[33,1536]{1,0:T(8,128)(2,1)S(1)}, bf16[33,1536]{1,0:T(8,128)(2,1)S(1)}, u32[]{:S(2)}, u32[]{:S(2)}) collective-permute-start(bf16[33,1536]{1,0:T(8,128)(2,1)S(1)} %fusion.8), channel_id=1, source_target_pairs={{0,1},{1,0},{2,3},{3,2},{4,5},{5,4},{6,7},{7,6},{8,9},{9,8},{10,11... | collective-permute-start | bytes 304136 | tf_op jit(solution)/shard_map/ppermute | solution.py:62
  23.2 14.4 %all-to-all-start.1 = ((bf16[16,32,512]{2,1,0:T(8,128)(2,1)}), bf16[16,32,512]{2,1,0:T(8,128)(2,1)S(1)}, u32[]{:S(2)}, u32[]{:S(2)}) async-start(bf16[16,32,512]{2,1,0:T(8,128)(2,1)} %broadcast_in_dim.59), calls=%async_computation.1 | async-start | bytes 1048576 | tf_op jit(solution)/shard_map/all_to_all | solution.py:46
  31.4 10.9 %copy-start.2 = (bf16[4,64,512]{2,1,0:T(8,128)(2,1)S(1)}, bf16[4,64,512]{2,1,0:T(8,128)(2,1)}, u32[]{:S(2)}) copy-start(bf16[4,64,512]{2,1,0:T(8,128)(2,1)} %param.17) | copy-start | bytes 786436
  31.4 11.4 %copy-start.1 = (bf16[32,64,128]{2,1,0:T(8,128)(2,1)S(1)}, bf16[32,64,128]{2,1,0:T(8,128)(2,1)}, u32[]{:S(2)}) copy-start(bf16[32,64,128]{2,1,0:T(8,128)(2,1)} %param.12) | copy-start | bytes 1572868
  32.5 9.8 %copy-start.4 = (bf16[4,64,512]{2,1,0:T(8,128)(2,1)S(1)}, bf16[4,64,512]{2,1,0:T(8,128)(2,1)}, u32[]{:S(2)}) copy-start(bf16[4,64,512]{2,1,0:T(8,128)(2,1)} %param.19) | copy-start | bytes 786436
  32.5 10.2 %copy-start.3 = (f32[32,8,64]{2,1,0:T(8,128)S(1)}, f32[32,8,64]{2,1,0:T(8,128)}, u32[]{:S(2)}) copy-start(f32[32,8,64]{2,1,0:T(8,128)} %fusion.50) | copy-start | bytes 196612
  38.3 3.6 %collective-permute-start.2 = (bf16[4,8,512]{2,1,0:T(8,128)(2,1)S(1)}, bf16[4,8,512]{2,1,0:T(8,128)(2,1)S(1)}, u32[]{:S(2)}, u32[]{:S(2)}) collective-permute-start(bf16[4,8,512]{2,1,0:T(8,128)(2,1)S(1)} %bitcast_select_fusion.1), channel_id=1, source_target_pairs={{0,1},{1,0},{2,3},{3,2},{4,5},{5,4},{6,7},{7,6},{8,9},{9,8},{10,11... | collective-permute-start | bytes 98312 | tf_op jit(solution)/shard_map/ppermute | solution.py:108

commit v6 on v1

--- a/solution.py
+++ b/solution.py
@@ -75,9 +75,9 @@
         high = jnp.where(even, t - leaf_count, t + leaf_count)
         return jnp.where(t < 0, low, jnp.where(t < leaf_count, t + leaf_count, high))
 
-    near_rows = jnp.take(density_padded, halo_row(near_list), axis=0).reshape(
-        leaf_count, near_list.shape[1], rhs_count, leaf_width
-    )
+    near_rows = jnp.take(
+        density_padded.reshape(-1, rhs_count, leaf_width), halo_row(near_list).reshape(-1), axis=0
+    ).reshape(leaf_count, near_list.shape[1], rhs_count, leaf_width)
     near_part = jnp.einsum(
         "ljpq,ljrq->lrp", near_blocks, near_rows, preferred_element_type=jnp.float32
     )

time: 44 us -> 46 us (1.045)
  other arithmetic: 2.67 us -> 3.58 us
  matrix products: 9.73 us -> 10.6 us
    dot_general x1, matrix products: 0.29 us -> 1.24 us  [body(): jnp.einsum('crk,ckq->crq', coarse_field, transfer, preferred_element_type...]
    convert_element_type x1, other arithmetic: 0.02 us -> 0.92 us  [body(): local_field = (leaf_far + descended).astype(jnp.bfloat16)]
    unnamed x12 -> x9, local copies, waits for them, and re-layouts: 0.94 us -> 0.91 us
  transfers between devices with their start and end apart: 5 -> 5, of which waited for: 2 -> 2; matrix products, arithmetic and copies ran while one was open for 33% -> 31% of each run, Pallas kernels for 0% -> 0%
where the time goes in v6:
time: 46 us; the launch traced here: 45.4 us
  starting transfers between devices  22.2 us (48%)
  matrix products  10.6 us (23%)
  local copies, waits for them, and re-layouts  7.59 us (16%)
  other arithmetic  3.58 us (8%)
  waiting for transfers between devices  1.17 us (3%)
    all_to_all x2, starting transfers between devices, body(): moved = lax.all_to_all(spread, axes, 0, 0, tiled=False)  13.7 us
    ppermute x1, starting transfers between devices, body(): cross = lax.ppermute(own, ALL, cross_pairs)  5.66 us
    dot_general x1, matrix products, body(): jnp.einsum('ljpq,ljrq->lrp', near_blocks, near_rows, preferred_element_ty...  4.54 us
    ppermute x1, starting transfers between devices, body(): lax.ppermute(jnp.take(everything, asked, axis=0), PAIR, [(0, 1), (1, 0)])  2.7 us
    broadcast_in_dim x4, local copies, waits for them, and re-layouts, body(): spread = jnp.broadcast_to(everything[None], (n,) + everything.shape)  1.59 us
    dot_general x1, matrix products, body(): jnp.einsum('lrp,lkp->lrk', density, basis, preferred_element_type=jnp.flo...  1.56 us
    dot_general x1, matrix products, body(): jnp.einsum('lkq,lrq->lrk', leaf_coupling, side_by_side(far_skels), prefer...  1.3 us
    dot_general x1, matrix products, body(): jnp.einsum('crk,ckq->crq', coarse_field, transfer, preferred_element_type...  1.24 us
  transfers between devices with their start and end apart: 5, of which 2 were waited for; matrix products, arithmetic and copies ran while one was open for 31% of the time, Pallas kernels for 0%

profile of v6, /device:TPU:1, one launch (start us, length us, event | category | flops | bytes accessed | tf_op | source)
XLA Modules:
  0.0 45.4 jit_solution(14700437701489356126)
XLA Ops:
  0.0 1.6 %convolution_convert_fusion = bf16[32,8,64]{2,1,0:T(8,128)(2,1)S(1)} fusion(bf16[32,8,128]{2,1,0:T(8,128)(2,1)} %param.11, bf16[32,64,128]{2,1,0:T(8,128)(2,1)} %param.12), kind=kOutput, calls=%fused_computation.7 | convolution fusion | flops 4210688 | bytes 622592 | tf_op jit(solution)/shard_map/lrp,lkp->lrk/dot_general | solution.py:34
  1.7 1.1 %convolution_convert_fusion.2 = bf16[4,8,64]{2,1,0:T(8,128)(2,1)S(1)} fusion(bf16[4,8,512]{2,1,0:T(8,128)(2,1)S(1)} %reshape.118, bf16[4,64,512]{2,1,0:T(8,128)(2,1)} %param.17), kind=kOutput, calls=%fused_computation.9 | convolution fusion | flops 2099200 | bytes 299008 | tf_op jit(solution)/shard_map/ckq,crq->crk/dot_general | solution.py:38
  2.9 0.6 %broadcast_in_dim.55 = bf16[8,4,512]{2,1,0:T(4,128)(2,1)} broadcast(bf16[4,512]{1,0:T(4,128)(2,1)S(1)} %broadcast_in_dim.54), dimensions={1,2} | broadcast | bytes 36864 | tf_op jit(solution)/shard_map/broadcast_in_dim | solution.py:45
  3.6 9.0 %all-to-all-start = ((bf16[8,4,512]{2,1,0:T(4,128)(2,1)}), bf16[8,4,512]{2,1,0:T(4,128)(2,1)S(1)}, u32[]{:S(2)}, u32[]{:S(2)}) async-start(bf16[8,4,512]{2,1,0:T(4,128)(2,1)} %broadcast_in_dim.55), calls=%async_computation | async-start | bytes 65536 | tf_op jit(solution)/shard_map/all_to_all | solution.py:46
  12.7 0.8 %bitcast_dynamic-update-slice_fusion = bf16[32,1536]{1,0:T(8,128)(2,1)S(1)} fusion(bf16[4,8,8,128]{3,2,1,0:T(8,128)(2,1)} %bitcast.55), kind=kLoop, calls=%fused_computation.24 | loop fusion | bytes 131072
  13.6 5.7 %collective-permute-start.1 = (bf16[32,1536]{1,0:T(8,128)(2,1)S(1)}, bf16[32,1536]{1,0:T(8,128)(2,1)S(1)}, u32[]{:S(2)}, u32[]{:S(2)}) collective-permute-start(bf16[32,1536]{1,0:T(8,128)(2,1)S(1)} %constant_dynamic-update-slice_fusion), channel_id=1, source_target_pairs={{1,2},{3,4},{5,6},{7,8},{9,10},{11,12},{13,14},{15,16},{17,18},{19... | collective-permute-start | bytes 294920 | tf_op jit(solution)/shard_map/ppermute | solution.py:61
  19.2 0.7 %fusion.48 = (bf16[1,4,8]{2,1,0:T(4,128)(2,1)S(1)}, bf16[1,4,8]{2,1,0:T(4,128)(2,1)S(1)}) fusion(s32[4,8]{1,0:T(4,128)} %param.18), kind=kLoop, calls=%fused_computation.154 | loop fusion | flops 672 | bytes 256 | tf_op jit(solution)/shard_map/stack | solution.py:57
  20.1 0.7 %compare_and_fusion.2 = (pred[4,8]{1,0:T(4,128)(4,1)S(1)}, s32[4,8]{1,0:T(4,128)S(1)}, pred[4,8]{1,0:T(4,128)(4,1)S(1)}) fusion(s32[4,8]{1,0:T(4,128)} %param.18, s32[]{:T(128)S(6)} %axis_index.60), kind=kLoop, calls=%fused_computation.145 | loop fusion | flops 3872 | bytes 324 | tf_op jit(solution)/shard_map/jit(_take)/and | solution.py:108
  21.0 0.7 %compare_and_fusion = (pred[32,6]{0,1:T(8,128)(4,1)S(1)}, s32[32,6]{0,1:T(8,128)S(1)}, pred[32,6]{0,1:T(8,128)(4,1)S(1)}, s32[32,6]{0,1:T(8,128)S(1)}) fusion(pred[]{:T(512)S(6)} %eq.16, s32[32,6]{0,1:T(8,128)} %param.15, s32[]{:T(128)S(6)} %mul.49, s32[32,6]{0,1:T(8,128)} %param.13), kind=kLoop, calls=%fused_computation.42 | loop fusion | flops 6144 | bytes 3461 | tf_op jit(solution)/shard_map/jit(_take)/and | solution.py:84
  22.4 0.8 %broadcast_in_dim.57 = bf16[16,32,512]{2,1,0:T(8,128)(2,1)} broadcast(bf16[32,512]{1,0:T(8,128)(2,1)S(1)} %broadcast_in_dim.56), dimensions={1,2} | broadcast | bytes 557056 | tf_op jit(solution)/shard_map/broadcast_in_dim | solution.py:45
  23.2 4.7 %all-to-all-start.1 = ((bf16[16,32,512]{2,1,0:T(8,128)(2,1)}), bf16[16,32,512]{2,1,0:T(8,128)(2,1)S(1)}, u32[]{:S(2)}, u32[]{:S(2)}) async-start(bf16[16,32,512]{2,1,0:T(8,128)(2,1)} %broadcast_in_dim.57), calls=%async_computation.1 | async-start | bytes 1048576 | tf_op jit(solution)/shard_map/all_to_all | solution.py:46
  28.4 1.0 %gather_fusion.1 = bf16[192,512]{1,0:T(8,128)(2,1)S(1)} fusion(bf16[96,512]{1,0:T(8,128)(2,1)S(1)} %pad_maximum_fusion.1, s32[1024]{0:T(1024)S(1)} %pad_clamp_fusion.2), kind=kCustom, calls=%fused_computation.3 | custom fusion | bytes 393984 | tf_op jit(solution)/shard_map/jit(_take)/gather | solution.py:84
  29.7 0.3 reshape.124
  30.1 1.3 %fusion.51 = f32[32,8,64]{2,1,0:T(8,128)} fusion(bf16[32,8,384]{2,1,0:T(8,128)(2,1)S(1)} %reshape.124, bf16[32,64,384]{2,1,0:T(8,128)(2,1)S(1)} %copy-done), kind=kOutput, calls=%fused_computation.158 | convolution fusion | flops 12582912 | bytes 1835008 | tf_op jit(solution)/shard_map/lkq,lrq->lrk/dot_general | solution.py:87
  31.4 0.7 %gather_fusion = bf16[192,8,128]{2,1,0:T(8,128)(2,1)S(1)} fusion(bf16[96,8,128]{2,1,0:T(8,128)(2,1)S(1)} %bitcast.52, s32[1024]{0:T(1024)S(1)} %pad_clamp_fusion.3), kind=kCustom, calls=%fused_computation.2 | custom fusion | bytes 787200 | tf_op jit(solution)/shard_map/jit(_take)/gather | solution.py:78
  32.2 4.5 %convolution_bitcast_fusion = f32[32,8,128]{2,1,0:T(8,128)S(1)} fusion(bf16[32,6,128,128]{3,2,1,0:T(8,128)(2,1)} %param.14, bf16[32,6,8,128]{3,2,1,0:T(8,128)(2,1)S(1)} %bitcast.53, pred[32,6]{1,0:T(8,128)(4,1)S(1)} %copy.23), kind=kOutput, calls=%fused_computation.5 | convolution fusion | flops 50528256 | bytes 6815936 | tf_op jit(solution)/shard_map/ljpq,ljrq->lrp/dot_general | solution.py:81
  36.7 0.9 %all-to-all-done.1 = bf16[16,32,512]{2,1,0:T(8,128)(2,1)S(1)} async-done(((bf16[16,32,512]{2,1,0:T(8,128)(2,1)}), bf16[16,32,512]{2,1,0:T(8,128)(2,1)S(1)}, u32[]{:S(2)}, u32[]{:S(2)}) %all-to-all-start.1) | async-done | bytes 524320 | tf_op jit(solution)/shard_map/all_to_all | solution.py:46
  37.7 0.6 %gather_fusion.2 = bf16[32,512]{1,0:T(8,128)(2,1)S(1)} fusion(bf16[512,512]{1,0:T(8,128)(2,1)S(1)} %bitcast.50, s32[1024]{0:T(1024)S(1)} %pad_clamp_fusion.1), kind=kCustom, calls=%fused_computation.clone | custom fusion | bytes 65664 | tf_op jit(solution)/shard_map/jit(_take)/gather | solution.py:106
  38.4 2.7 %collective-permute-start.2 = (bf16[4,8,512]{2,1,0:T(8,128)(2,1)S(1)}, bf16[4,8,512]{2,1,0:T(8,128)(2,1)S(1)}, u32[]{:S(2)}, u32[]{:S(2)}) collective-permute-start(bf16[4,8,512]{2,1,0:T(8,128)(2,1)S(1)} %bitcast_select_fusion.1), channel_id=1, source_target_pairs={{0,1},{1,0},{2,3},{3,2},{4,5},{5,4},{6,7},{7,6},{8,9},{9,8},{10,11... | collective-permute-start | bytes 98312 | tf_op jit(solution)/shard_map/ppermute | solution.py:106
  41.1 0.6 %gather_fusion.3 = bf16[32,512]{1,0:T(8,128)(2,1)S(1)} fusion(bf16[512,512]{1,0:T(8,128)(2,1)S(1)} %bitcast.51, s32[1024]{0:T(1024)S(1)} %pad_clamp_fusion), kind=kCustom, calls=%fused_computation.1.clone | custom fusion | bytes 65664 | tf_op jit(solution)/shard_map/jit(_take)/gather | solution.py:108
  41.7 0.2 collective-permute-done.2
  42.2 1.2 %fusion.1 = f32[4,8,512]{2,1,0:T(8,128)S(1)} fusion(bf16[4,64,512]{2,1,0:T(8,128)(2,1)S(1)} %copy-done.2, bf16[4,8,512]{2,1,0:T(8,128)(2,1)S(1)} %reshape.126, bf16[4,64,512]{2,1,0:T(8,128)(2,1)} %param.19), kind=kOutput, calls=%fused_computation.10 | convolution fusion | flops 4196352 | bytes 622592 | tf_op jit(solution)/shard_map/crk,ckq->crq/dot_general | solution.py:113
  43.6 0.9 %fusion.7 = bf16[32,8,64]{2,1,0:T(8,128)(2,1)S(1)} fusion(f32[32,8,64]{2,1,0:T(8,128)} %fusion.51, f32[4,8,8,64]{3,1,2,0:T(8,128)S(1)} %copy.29), kind=kLoop, calls=%fused_computation.21 | loop fusion | flops 32768 | bytes 163840 | tf_op jit(solution)/shard_map/convert_element_type | solution.py:121
  44.6 0.9 %fusion = bf16[32,8,128]{2,1,0:T(8,128)(2,1)} fusion(f32[32,8,128]{2,1,0:T(8,128)S(1)} %convolution_bitcast_fusion, bf16[32,8,64]{2,1,0:T(8,128)(2,1)S(1)} %fusion.7, bf16[32,64,128]{2,1,0:T(8,128)(2,1)S(1)} %copy-done.1), kind=kOutput, calls=%fused_computation.6 | convolution fusion | flops 4259840 | bytes 753664 | tf_op jit(solution)/shard_map/lrk,lkp->lrp/dot_general | solution.py:123
  (50 shorter events, 2.5 us)
Async XLA Ops:
  0.0 30.1 %copy-start = (bf16[32,64,384]{2,1,0:T(8,128)(2,1)S(1)}, bf16[32,64,384]{2,1,0:T(8,128)(2,1)}, u32[]{:S(2)}) copy-start(bf16[32,64,384]{2,1,0:T(8,128)(2,1)} %param.16) | copy-start | bytes 4718596
  3.6 18.8 %all-to-all-start = ((bf16[8,4,512]{2,1,0:T(4,128)(2,1)}), bf16[8,4,512]{2,1,0:T(4,128)(2,1)S(1)}, u32[]{:S(2)}, u32[]{:S(2)}) async-start(bf16[8,4,512]{2,1,0:T(4,128)(2,1)} %broadcast_in_dim.55), calls=%async_computation | async-start | bytes 65536 | tf_op jit(solution)/shard_map/all_to_all | solution.py:46
  13.6 14.7 %collective-permute-start.1 = (bf16[32,1536]{1,0:T(8,128)(2,1)S(1)}, bf16[32,1536]{1,0:T(8,128)(2,1)S(1)}, u32[]{:S(2)}, u32[]{:S(2)}) collective-permute-start(bf16[32,1536]{1,0:T(8,128)(2,1)S(1)} %constant_dynamic-update-slice_fusion), channel_id=1, source_target_pairs={{1,2},{3,4},{5,6},{7,8},{9,10},{11,12},{13,14},{15,16},{17,18},{19... | collective-permute-start | bytes 294920 | tf_op jit(solution)/shard_map/ppermute | solution.py:61
  20.0 7.9 %collective-permute-start = (bf16[33,1536]{1,0:T(8,128)(2,1)S(1)}, bf16[33,1536]{1,0:T(8,128)(2,1)S(1)}, u32[]{:S(2)}, u32[]{:S(2)}) collective-permute-start(bf16[33,1536]{1,0:T(8,128)(2,1)S(1)} %fusion.8), channel_id=1, source_target_pairs={{0,1},{1,0},{2,3},{3,2},{4,5},{5,4},{6,7},{7,6},{8,9},{9,8},{10,11... | collective-permute-start | bytes 304136 | tf_op jit(solution)/shard_map/ppermute | solution.py:62
  23.2 14.4 %all-to-all-start.1 = ((bf16[16,32,512]{2,1,0:T(8,128)(2,1)}), bf16[16,32,512]{2,1,0:T(8,128)(2,1)S(1)}, u32[]{:S(2)}, u32[]{:S(2)}) async-start(bf16[16,32,512]{2,1,0:T(8,128)(2,1)} %broadcast_in_dim.57), calls=%async_computation.1 | async-start | bytes 1048576 | tf_op jit(solution)/shard_map/all_to_all | solution.py:46
  29.6 12.7 %copy-start.2 = (bf16[4,64,512]{2,1,0:T(8,128)(2,1)S(1)}, bf16[4,64,512]{2,1,0:T(8,128)(2,1)}, u32[]{:S(2)}) copy-start(bf16[4,64,512]{2,1,0:T(8,128)(2,1)} %param.17) | copy-start | bytes 786436
  30.1 14.5 %copy-start.1 = (bf16[32,64,128]{2,1,0:T(8,128)(2,1)S(1)}, bf16[32,64,128]{2,1,0:T(8,128)(2,1)}, u32[]{:S(2)}) copy-start(bf16[32,64,128]{2,1,0:T(8,128)(2,1)} %param.12) | copy-start | bytes 1572868
  38.4 3.6 %collective-permute-start.2 = (bf16[4,8,512]{2,1,0:T(8,128)(2,1)S(1)}, bf16[4,8,512]{2,1,0:T(8,128)(2,1)S(1)}, u32[]{:S(2)}, u32[]{:S(2)}) collective-permute-start(bf16[4,8,512]{2,1,0:T(8,128)(2,1)S(1)} %bitcast_select_fusion.1), channel_id=1, source_target_pairs={{0,1},{1,0},{2,3},{3,2},{4,5},{5,4},{6,7},{7,6},{8,9},{9,8},{10,11... | collective-permute-start | bytes 98312 | tf_op jit(solution)/shard_map/ppermute | solution.py:106
